TPU v7x, 128 devices: a whole 4x4x4 slice. The times are simulated.
128 devices in a mesh: blk: 16 (over x_lo, y, core), col: 8 (over x_hi, z).
Axes of the slice: x: 4 (x_hi: 2, x_lo: 2; x = x_hi * 2 + x_lo), y: 4, z: 4, core: 2. Of those that a mesh axis runs over, the one named last changes fastest.
Arguments:
- queries: bfloat16 [2048, 384], P('blk', 'col'), may hold values from -8 to 8
- key_proj: bfloat16 [2048, 384], P('blk', 'col'), may hold values from -8 to 8
- value_proj: bfloat16 [2048, 384], P('blk', 'col'), may hold values from -6 to 6
- out_grad: bfloat16 [2048, 384], P('blk', 'col'), may hold values from -12 to 12
- pair_rep: bfloat16 [2048, 2048, 128], P('blk', 'col'), may hold values from -600 to 600
- norm_gain: float32 [128], replicated, may hold values from 0.1 to 1.9
- bias_weight: bfloat16 [128, 16], replicated, may hold values from -1 to 1
- chain_ids: int32 [2048], replicated, may hold values from 0 to 15, never falling along the last dimension, each value on 1 to 512 neighbouring positions
- block_mask: int32 [16, 16], replicated, may hold values 0 or 1
Outputs:
- grad_queries: bfloat16 [2048, 384], P('blk', 'col')
- grad_keys: bfloat16 [2048, 384], P('blk', 'col')
- grad_values: bfloat16 [2048, 384], P('blk', 'col')
- grad_pair: bfloat16 [2048, 2048, 128], P('blk', 'col')
- grad_gain: float32 [128], replicated
- grad_weight: float32 [128, 16], replicated
Inputs may be any that keep to these rules, and one draw needn't show every extreme that they name: `chain_ids`: chain ids never fall along the tokens; every chain has 1 to 512 tokens and one has exactly 512.
All inputs are finite; a program needn't handle non-finite values.
Results may differ from a plain program's by a relative error of at most 0.02.
Values may be sent and summed in bfloat16 or wider, within the bound.
No kernel may reach another device: no remote copies, remote signals or barrier semaphores. Data moves between devices by JAX's collectives and lax.ppermute only.
A program may use at most 192 MiB of HBM per device.

v0:
```python
import math

import jax
import jax.numpy as jnp
from jax import lax
from jax.sharding import PartitionSpec as P

HEAD_DIM = 24
MASK_BLOCK = 128


def from_behind(block, axis, distance):
    devices = range(lax.axis_size(axis))
    route = [((i - distance) % len(devices), i) for i in devices]
    return lax.ppermute(block, axis, route)


def pair_norm(pair_rows, norm_gain):
    values = pair_rows.astype(jnp.float32)
    centre = jnp.mean(values, axis=-1, keepdims=True)
    shifted = values - centre
    inverse = lax.rsqrt(jnp.mean(shifted * shifted, axis=-1, keepdims=True) + 1e-05)
    unit = shifted * inverse
    normed = (unit * norm_gain).astype(jnp.bfloat16)
    return (unit, inverse, normed)


def block_onehot(first_token, count, nblocks):
    block_ids = (first_token + jnp.arange(count, dtype=jnp.int32)) // MASK_BLOCK
    return (block_ids[:, None] == jnp.arange(nblocks, dtype=jnp.int32)[None, :]).astype(
        jnp.bfloat16
    )


def pass_grads(grads):
    return from_behind(grads, "blk", 1)


def local(
    queries, key_proj, value_proj, out_grad, pair_rep, norm_gain, bias_weight, chain_ids, block_mask
):
    tok_rows = queries.shape[0]
    local_width = queries.shape[1]
    local_heads = local_width // HEAD_DIM
    scale_factor = 1.0 / math.sqrt(HEAD_DIM)
    blk_index = lax.axis_index("blk")
    blk_count = lax.axis_size("blk")
    all_tokens = blk_count * tok_rows
    row_start = blk_index * tok_rows
    nblocks = block_mask.shape[0]
    rows_table = jnp.dot(
        block_onehot(row_start, tok_rows, nblocks),
        block_mask.astype(jnp.bfloat16),
        preferred_element_type=jnp.float32,
    ).astype(jnp.bfloat16)
    chain_rows = lax.dynamic_slice_in_dim(chain_ids, row_start, tok_rows)

    def tile_allowed(col_start, count):
        hits = lax.dot_general(
            rows_table,
            block_onehot(col_start, count, nblocks),
            (((1,), (1,)), ((), ())),
            preferred_element_type=jnp.float32,
        )
        chain_cols = lax.dynamic_slice_in_dim(chain_ids, col_start, count)
        return (hits > 0.5) | (chain_rows[:, None] == chain_cols[None, :])

    unit, inverse, normed = pair_norm(pair_rep, norm_gain)
    kv_local = jnp.stack([key_proj, value_proj])
    query_heads = queries.reshape(tok_rows, local_heads, HEAD_DIM)
    grad_heads = out_grad.reshape(tok_rows, local_heads, HEAD_DIM)
    bias_local = jnp.einsum(
        "ijc,ch->hij", normed, bias_weight, preferred_element_type=jnp.float32
    ).astype(jnp.bfloat16)
    bias_mine = lax.all_to_all(bias_local, "col", split_axis=0, concat_axis=2, tiled=True)

    def tile_scores(kv_piece, col_start, count):
        key_heads = kv_piece[0].reshape(count, local_heads, HEAD_DIM)
        value_heads = kv_piece[1].reshape(count, local_heads, HEAD_DIM)
        bias_part = lax.dynamic_slice_in_dim(bias_mine, col_start, count, 2).astype(jnp.float32)
        scores = (
            jnp.einsum("qhd,khd->hqk", query_heads, key_heads, preferred_element_type=jnp.float32)
            * scale_factor
            + bias_part
        )
        return (key_heads, value_heads, scores)

    def forward_tile(stats, kv_piece, col_start):
        count = kv_piece.shape[1]
        allowed = tile_allowed(col_start, count)
        running_max, totals, accum = stats
        key_heads, value_heads, scores = tile_scores(kv_piece, col_start, count)
        masked = jnp.where(allowed[None], scores, -jnp.inf)
        new_max = jnp.maximum(running_max, jnp.max(masked, axis=-1))
        expo = jnp.where(allowed[None], jnp.exp(scores - new_max[:, :, None]), 0.0)
        factor = jnp.exp(running_max - new_max)
        totals = totals * factor + jnp.sum(expo, axis=-1)
        accum = accum * factor.T[:, :, None] + jnp.einsum(
            "hqk,khd->qhd", expo, value_heads.astype(jnp.float32)
        )
        return (new_max, totals, accum)

    stats_init = (
        jnp.full((local_heads, tok_rows), -1e30, jnp.float32),
        jnp.zeros((local_heads, tok_rows), jnp.float32),
        jnp.zeros((tok_rows, local_heads, HEAD_DIM), jnp.float32),
    )
    first_stats = forward_tile(stats_init, kv_local, row_start)

    def cycle_forward(turn, loop_state):
        stats_now, kv_now = loop_state
        kv_now = from_behind(kv_now, "blk", 1)
        source = (blk_index - turn) % blk_count
        return (forward_tile(stats_now, kv_now, source * tok_rows), kv_now)

    stats_done, kv_final = lax.fori_loop(1, blk_count, cycle_forward, (first_stats, kv_local))
    running_max, totals, accum = stats_done
    log_total = running_max + jnp.log(totals)
    attended = accum / totals.T[:, :, None]
    delta = jnp.sum(grad_heads.astype(jnp.float32) * attended, axis=-1).T

    def backward_tile(kv_piece, col_start):
        count = kv_piece.shape[1]
        allowed = tile_allowed(col_start, count)
        key_heads, value_heads, scores = tile_scores(kv_piece, col_start, count)
        probs = jnp.where(allowed[None], jnp.exp(scores - log_total[:, :, None]), 0.0).astype(
            jnp.bfloat16
        )
        dprobs = jnp.einsum(
            "qhd,khd->hqk", grad_heads, value_heads, preferred_element_type=jnp.float32
        )
        dscores = (probs.astype(jnp.float32) * (dprobs - delta[:, :, None])).astype(jnp.bfloat16)
        query_add = (
            jnp.einsum("hqk,khd->qhd", dscores, key_heads, preferred_element_type=jnp.float32)
            * scale_factor
        )
        key_add = (
            jnp.einsum("hqk,qhd->khd", dscores, query_heads, preferred_element_type=jnp.float32)
            * scale_factor
        )
        value_add = jnp.einsum(
            "hqk,qhd->khd", probs, grad_heads, preferred_element_type=jnp.float32
        )
        return (
            dscores,
            query_add,
            jnp.stack([key_add.reshape(count, local_width), value_add.reshape(count, local_width)]),
        )

    dbias_init = jnp.zeros((local_heads, tok_rows, all_tokens), jnp.bfloat16)
    first_scores, first_query, first_kv = backward_tile(kv_local, row_start)
    first_bias = lax.dynamic_update_slice_in_dim(dbias_init, first_scores, row_start, 2)

    def cycle_backward(turn, loop_state):
        query_acc, kv_acc, kv_now, dbias = loop_state
        kv_now = from_behind(kv_now, "blk", 1)
        kv_acc = pass_grads(kv_acc)
        source = (blk_index - turn) % blk_count
        dscores, query_add, kv_add = backward_tile(kv_now, source * tok_rows)
        dbias = lax.dynamic_update_slice_in_dim(dbias, dscores, source * tok_rows, 2)
        return (query_acc + query_add, kv_acc + kv_add, kv_now, dbias)

    query_acc, kv_acc, kv_final, dbias = lax.fori_loop(
        1, blk_count, cycle_backward, (first_query, first_kv, kv_local, first_bias)
    )
    kv_grads = pass_grads(kv_acc)
    grad_queries = query_acc.reshape(tok_rows, local_width).astype(jnp.bfloat16)
    grad_keys = kv_grads[0].astype(jnp.bfloat16)
    grad_values = kv_grads[1].astype(jnp.bfloat16)
    dbias_cells = lax.all_to_all(dbias, "col", split_axis=2, concat_axis=0, tiled=True)
    dnormed = jnp.einsum(
        "hij,ch->ijc", dbias_cells, bias_weight, preferred_element_type=jnp.float32
    )
    gain_part = jnp.sum(dnormed * unit, axis=(0, 1))
    weight_part = jnp.einsum("ijc,hij->ch", normed, dbias_cells, preferred_element_type=jnp.float32)
    grad_weight, grad_gain = lax.psum((weight_part, gain_part), ("blk", "col"))
    scaled = dnormed * norm_gain
    grad_pair = (
        inverse
        * (
            scaled
            - jnp.mean(scaled, axis=-1, keepdims=True)
            - unit * jnp.mean(scaled * unit, axis=-1, keepdims=True)
        )
    ).astype(jnp.bfloat16)
    return (grad_queries, grad_keys, grad_values, grad_pair, grad_gain, grad_weight)


def solution(mesh):
    placed = (
        P("blk", "col"),
        P("blk", "col"),
        P("blk", "col"),
        P("blk", "col"),
        P("blk", "col", None),
        P(),
        P(),
        P(),
        P(),
    )
    return jax.shard_map(
        local,
        mesh=mesh,
        in_specs=placed,
        out_specs=(
            P("blk", "col"),
            P("blk", "col"),
            P("blk", "col"),
            P("blk", "col", None),
            P(),
            P(),
        ),
        check_vma=False,
    )
```

profile of v0, /device:TPU:1, one launch (start us, length us, event | category | flops | bytes accessed | tf_op | source)
XLA Modules:
  0.0 363.6 jit_solution(301229899004994929)
XLA Ops:
  0.7 11.9 %copy.34 = bf16[128,256,128]{1,2,0:T(8,128)(2,1)} copy(bf16[128,256,128]{2,1,0:T(8,128)(2,1)} %param.17) | data formatting | bytes 16777216 | tf_op args[4]
  12.6 6.1 %convert_reduce_fusion = f32[128,256]{1,0:T(8,128)S(1)} fusion(bf16[128,256,128]{1,2,0:T(8,128)(2,1)} %copy.34), kind=kLoop, calls=%fused_computation.49 | loop fusion | flops 8355840 | bytes 8519680 | tf_op jit(solution)/shard_map/reduce_sum | solution.py:20
  18.7 7.3 %fusion.35 = f32[128,256]{1,0:T(8,128)S(1)} fusion(bf16[128,256,128]{1,2,0:T(8,128)(2,1)} %copy.34, f32[128,256]{1,0:T(8,128)S(1)} %broadcast_multiply_fusion.2), kind=kLoop, calls=%fused_computation.62 | loop fusion | flops 16744448 | bytes 8650752 | tf_op jit(solution)/shard_map/reduce_sum | solution.py:22
  30.1 8.3 %all-to-all-start = ((bf16[16,128,256]{2,1,0:T(8,128)(2,1)}), bf16[16,128,256]{2,1,0:T(8,128)(2,1)S(1)}, u32[]{:S(2)}, u32[]{:S(2)}) async-start(bf16[16,128,256]{2,1,0:T(8,128)(2,1)} %copy.36), calls=%async_computation | async-start | bytes 2097152 | tf_op jit(solution)/shard_map/all_to_all | solution.py:75
  39.8 12.8 %all-to-all-done = bf16[16,128,256]{2,1,0:T(8,128)(2,1)S(1)} async-done(((bf16[16,128,256]{2,1,0:T(8,128)(2,1)}), bf16[16,128,256]{2,1,0:T(8,128)(2,1)S(1)}, u32[]{:S(2)}, u32[]{:S(2)}) %all-to-all-start) | async-done | bytes 1048608 | tf_op jit(solution)/shard_map/all_to_all | solution.py:75
  53.8 86.8 %while.42 = (s32[]{:T(128)}, f32[2,128]{1,0:T(2,128)S(1)}, f32[2,128]{1,0:T(2,128)S(1)}, f32[128,2,24]{0,2,1:T(8,128)S(1)}, bf16[2,128,48]{1,2,0:T(8,128)(2,1)S(...) while((s32[]{:T(128)}, f32[2,128]{1,0:T(2,128)S(1)}, ...), condition=%wide.region_7.8_spmd, body=%wide.region_4.7_spmd.sunk | while | flops 4064018 | bytes 830840 | solution.py:116
  70.5 4.3 %collective-permute-done = bf16[2,128,48]{1,2,0:T(8,128)(2,1)S(1)} collective-permute-done((bf16[2,128,48]{1,2,0:T(8,128)(2,1)S(1)}, bf16[2,128,48]{1,2,0:T(8,128)(2,1)S(1)}, u32[]{:S(2)}, u32[]{:S(2)}) %collective-permute-start) | collective-permute-done | bytes 24608 | tf_op jit(solution)/shard_map/while/body/eval_jaxpr/ppermute | solution.py:15
  76.4 4.3 %collective-permute-done = bf16[2,128,48]{1,2,0:T(8,128)(2,1)S(1)} collective-permute-done((bf16[2,128,48]{1,2,0:T(8,128)(2,1)S(1)}, bf16[2,128,48]{1,2,0:T(8,128)(2,1)S(1)}, u32[]{:S(2)}, u32[]{:S(2)}) %collective-permute-start) | collective-permute-done | bytes 24608 | tf_op jit(solution)/shard_map/while/body/eval_jaxpr/ppermute | solution.py:15
  82.4 4.3 %collective-permute-done = bf16[2,128,48]{1,2,0:T(8,128)(2,1)S(1)} collective-permute-done((bf16[2,128,48]{1,2,0:T(8,128)(2,1)S(1)}, bf16[2,128,48]{1,2,0:T(8,128)(2,1)S(1)}, u32[]{:S(2)}, u32[]{:S(2)}) %collective-permute-start) | collective-permute-done | bytes 24608 | tf_op jit(solution)/shard_map/while/body/eval_jaxpr/ppermute | solution.py:15
  88.3 4.3 %collective-permute-done = bf16[2,128,48]{1,2,0:T(8,128)(2,1)S(1)} collective-permute-done((bf16[2,128,48]{1,2,0:T(8,128)(2,1)S(1)}, bf16[2,128,48]{1,2,0:T(8,128)(2,1)S(1)}, u32[]{:S(2)}, u32[]{:S(2)}) %collective-permute-start) | collective-permute-done | bytes 24608 | tf_op jit(solution)/shard_map/while/body/eval_jaxpr/ppermute | solution.py:15
  94.2 4.3 %collective-permute-done = bf16[2,128,48]{1,2,0:T(8,128)(2,1)S(1)} collective-permute-done((bf16[2,128,48]{1,2,0:T(8,128)(2,1)S(1)}, bf16[2,128,48]{1,2,0:T(8,128)(2,1)S(1)}, u32[]{:S(2)}, u32[]{:S(2)}) %collective-permute-start) | collective-permute-done | bytes 24608 | tf_op jit(solution)/shard_map/while/body/eval_jaxpr/ppermute | solution.py:15
  100.2 4.3 %collective-permute-done = bf16[2,128,48]{1,2,0:T(8,128)(2,1)S(1)} collective-permute-done((bf16[2,128,48]{1,2,0:T(8,128)(2,1)S(1)}, bf16[2,128,48]{1,2,0:T(8,128)(2,1)S(1)}, u32[]{:S(2)}, u32[]{:S(2)}) %collective-permute-start) | collective-permute-done | bytes 24608 | tf_op jit(solution)/shard_map/while/body/eval_jaxpr/ppermute | solution.py:15
  106.1 4.3 %collective-permute-done = bf16[2,128,48]{1,2,0:T(8,128)(2,1)S(1)} collective-permute-done((bf16[2,128,48]{1,2,0:T(8,128)(2,1)S(1)}, bf16[2,128,48]{1,2,0:T(8,128)(2,1)S(1)}, u32[]{:S(2)}, u32[]{:S(2)}) %collective-permute-start) | collective-permute-done | bytes 24608 | tf_op jit(solution)/shard_map/while/body/eval_jaxpr/ppermute | solution.py:15
  112.0 4.3 %collective-permute-done = bf16[2,128,48]{1,2,0:T(8,128)(2,1)S(1)} collective-permute-done((bf16[2,128,48]{1,2,0:T(8,128)(2,1)S(1)}, bf16[2,128,48]{1,2,0:T(8,128)(2,1)S(1)}, u32[]{:S(2)}, u32[]{:S(2)}) %collective-permute-start) | collective-permute-done | bytes 24608 | tf_op jit(solution)/shard_map/while/body/eval_jaxpr/ppermute | solution.py:15
  123.9 4.3 %collective-permute-done = bf16[2,128,48]{1,2,0:T(8,128)(2,1)S(1)} collective-permute-done((bf16[2,128,48]{1,2,0:T(8,128)(2,1)S(1)}, bf16[2,128,48]{1,2,0:T(8,128)(2,1)S(1)}, u32[]{:S(2)}, u32[]{:S(2)}) %collective-permute-start) | collective-permute-done | bytes 24608 | tf_op jit(solution)/shard_map/while/body/eval_jaxpr/ppermute | solution.py:15
  135.8 4.3 %collective-permute-done = bf16[2,128,48]{1,2,0:T(8,128)(2,1)S(1)} collective-permute-done((bf16[2,128,48]{1,2,0:T(8,128)(2,1)S(1)}, bf16[2,128,48]{1,2,0:T(8,128)(2,1)S(1)}, u32[]{:S(2)}, u32[]{:S(2)}) %collective-permute-start) | collective-permute-done | bytes 24608 | tf_op jit(solution)/shard_map/while/body/eval_jaxpr/ppermute | solution.py:15
  141.6 95.9 %while.43 = (s32[]{:T(128)}, f32[128,2,24]{0,2,1:T(8,128)S(1)}, f32[2,128,48]{1,2,0:T(8,128)S(1)}, bf16[2,128,48]{1,2,0:T(8,128)(2,1)S(1)}, bf16[2,128,2048]{2,1...) while((s32[]{:T(128)}, f32[128,2,24]{0,2,1:T(8,128)S(1)}, ...), condition=%wide.region_10.11_spmd, body=%wide.region_9.10_spmd.sunk | while | flops 8812562 | bytes 1586620 | solution.py:163
  244.0 5.0 %collective-permute-done.3 = bf16[2,128,48]{1,2,0:T(8,128)(2,1)S(1)} collective-permute-done((bf16[2,128,48]{1,2,0:T(8,128)(2,1)S(1)}, bf16[2,128,48]{1,2,0:T(8,128)(2,1)S(1)}, u32[]{:S(2)}, u32[]{:S(2)}) %collective-permute-start.3) | collective-permute-done | bytes 24608 | tf_op jit(solution)/shard_map/ppermute | solution.py:15
  249.7 4.6 %all-to-all-done.1 = bf16[2,128,2048]{1,0,2:T(2,128)(2,1)S(1)} async-done(((bf16[2,128,2048]{1,0,2:T(2,128)(2,1)}), bf16[2,128,2048]{1,0,2:T(2,128)(2,1)S(1)}, u32[]{:S(2)}, u32[]{:S(2)}) %all-to-all-start.1) | async-done | bytes 1048608 | tf_op jit(solution)/shard_map/all_to_all | solution.py:170
  256.8 6.2 %fusion.46 = f32[128,16]{0,1:T(8,128)S(1)} fusion(bf16[16,128,256]{2,0,1:T(8,128)(2,1)S(1)} %all_to_all.33, bf16[128,256,128]{1,2,0:T(8,128)(2,1)} %copy.34, f32[128]{0:T(128)S(1)} %copy-done.5, f32[128,256]{1,0:T(8,128)S(1)} %add_rsqrt_fusion, f32[128,256]{1,0:T(8,128)S(1)} %broadcast_multiply_fusion.2), kind=kOutput, calls=%fused_computation.79 | convolution fusion | flops 155189248 | bytes 9708032 | tf_op jit(solution)/shard_map/ijc,hij->ch/dot_general | solution.py:175
  263.0 8.9 %fusion.34 = (f32[128]{0:T(128)S(1)}, f32[128,256]{1,0:T(8,128)S(1)}, f32[128,256]{1,0:T(8,128)S(1)}, f32[128,256,128]{1,2,0:T(8,128)S(1)}) fusion(bf16[128,256,128]{1,2,0:T(8,128)(2,1)} %copy.34, f32[128,256]{1,0:T(8,128)S(1)} %add_rsqrt_fusion, f32[128,256]{1,0:T(8,128)S(1)} %broadcast_multiply_fusion.2, f32[128]{0:T(128)S(1)} %copy-done.5, ...), kind=kOutput, calls=%fused_computation.61 | convolution fusion | flops 171900800 | bytes 26743808 | tf_op jit(solution)/shard_map/hij,ch->ijc/dot_general | solution.py:171
  271.9 8.5 %fusion.33 = bf16[128,256,128]{1,2,0:T(8,128)(2,1)} fusion(bf16[128,256,128]{1,2,0:T(8,128)(2,1)S(1)} %bitcast.157, f32[128,256,128]{1,2,0:T(8,128)S(1)} %get-tuple-element.727, f32[128,256]{1,0:T(8,128)S(1)} %get-tuple-element.728, f32[128,256]{1,0:T(8,128)S(1)} %get-tuple-element.729, f32[128]{0:T(128)S(1)} %copy-done.5, f32[128,256]{1,0:T(8,128)S(1)} %add_rsqrt_fusion, ...), kind=kLoop, calls=%fused_computation.60 | loop fusion | flops 37748736 | bytes 34079232 | tf_op jit(solution)/shard_map/convert_element_type | solution.py:185
  280.4 11.9 %copy.48 = bf16[128,256,128]{2,1,0:T(8,128)(2,1)} copy(bf16[128,256,128]{1,2,0:T(8,128)(2,1)} %fusion.33) | data formatting | bytes 16777216
  292.4 71.2 %all-reduce = (f32[128]{0:T(128)}, f32[128,16]{0,1:T(8,128)}) all-reduce(f32[128]{0:T(128)S(1)} %get-tuple-element.656, f32[128,16]{0,1:T(8,128)S(1)} %fusion.46), channel_id=1, replica_groups=mesh['blk'=16,'col'=8] {'blk','col'}, use_global_device_ids=true, to_apply=%region_14.15 | all-reduce | flops 2176 | bytes 17408 | tf_op jit(solution)/shard_map/psum | solution.py:176
  (515 shorter events, 153.4 us)
Async XLA Ops:
  30.1 22.5 %all-to-all-start = ((bf16[16,128,256]{2,1,0:T(8,128)(2,1)}), bf16[16,128,256]{2,1,0:T(8,128)(2,1)S(1)}, u32[]{:S(2)}, u32[]{:S(2)}) async-start(bf16[16,128,256]{2,1,0:T(8,128)(2,1)} %copy.36), calls=%async_computation | async-start | bytes 2097152 | tf_op jit(solution)/shard_map/all_to_all | solution.py:75
  75.3 5.4 %collective-permute-start = (bf16[2,128,48]{1,2,0:T(8,128)(2,1)S(1)}, bf16[2,128,48]{1,2,0:T(8,128)(2,1)S(1)}, u32[]{:S(2)}, u32[]{:S(2)}) collective-permute-start(bf16[2,128,48]{1,2,0:T(8,128)(2,1)S(1)} %get-tuple-element.923), channel_id=1, source_target_pairs={{120,0},{0,8},{8,16},{16,24},{24,32},{32,40},{40,48},{48,56},{56,6... | collective-permute-start | bytes 73736 | tf_op jit(solution)/shard_map/while/body/eval_jaxpr/ppermute | solution.py:15
  99.1 5.4 %collective-permute-start = (bf16[2,128,48]{1,2,0:T(8,128)(2,1)S(1)}, bf16[2,128,48]{1,2,0:T(8,128)(2,1)S(1)}, u32[]{:S(2)}, u32[]{:S(2)}) collective-permute-start(bf16[2,128,48]{1,2,0:T(8,128)(2,1)S(1)} %get-tuple-element.923), channel_id=1, source_target_pairs={{120,0},{0,8},{8,16},{16,24},{24,32},{32,40},{40,48},{48,56},{56,6... | collective-permute-start | bytes 73736 | tf_op jit(solution)/shard_map/while/body/eval_jaxpr/ppermute | solution.py:15
  110.9 5.4 %collective-permute-start = (bf16[2,128,48]{1,2,0:T(8,128)(2,1)S(1)}, bf16[2,128,48]{1,2,0:T(8,128)(2,1)S(1)}, u32[]{:S(2)}, u32[]{:S(2)}) collective-permute-start(bf16[2,128,48]{1,2,0:T(8,128)(2,1)S(1)} %get-tuple-element.923), channel_id=1, source_target_pairs={{120,0},{0,8},{8,16},{16,24},{24,32},{32,40},{40,48},{48,56},{56,6... | collective-permute-start | bytes 73736 | tf_op jit(solution)/shard_map/while/body/eval_jaxpr/ppermute | solution.py:15
  122.8 5.4 %collective-permute-start = (bf16[2,128,48]{1,2,0:T(8,128)(2,1)S(1)}, bf16[2,128,48]{1,2,0:T(8,128)(2,1)S(1)}, u32[]{:S(2)}, u32[]{:S(2)}) collective-permute-start(bf16[2,128,48]{1,2,0:T(8,128)(2,1)S(1)} %get-tuple-element.923), channel_id=1, source_target_pairs={{120,0},{0,8},{8,16},{16,24},{24,32},{32,40},{40,48},{48,56},{56,6... | collective-permute-start | bytes 73736 | tf_op jit(solution)/shard_map/while/body/eval_jaxpr/ppermute | solution.py:15
  141.7 6.3 %collective-permute-start.2 = (f32[2,128,48]{1,2,0:T(8,128)S(1)}, f32[2,128,48]{1,2,0:T(8,128)S(1)}, u32[]{:S(2)}, u32[]{:S(2)}) collective-permute-start(f32[2,128,48]{1,2,0:T(8,128)S(1)} %get-tuple-element.975), channel_id=1, source_target_pairs={{120,0},{0,8},{8,16},{16,24},{24,32},{32,40},{40,48},{48,56},{56,6... | collective-permute-start | bytes 147464 | tf_op jit(solution)/shard_map/while/body/eval_jaxpr/ppermute | solution.py:15
  148.1 6.3 %collective-permute-start.2 = (f32[2,128,48]{1,2,0:T(8,128)S(1)}, f32[2,128,48]{1,2,0:T(8,128)S(1)}, u32[]{:S(2)}, u32[]{:S(2)}) collective-permute-start(f32[2,128,48]{1,2,0:T(8,128)S(1)} %get-tuple-element.975), channel_id=1, source_target_pairs={{120,0},{0,8},{8,16},{16,24},{24,32},{32,40},{40,48},{48,56},{56,6... | collective-permute-start | bytes 147464 | tf_op jit(solution)/shard_map/while/body/eval_jaxpr/ppermute | solution.py:15
  154.5 6.3 %collective-permute-start.2 = (f32[2,128,48]{1,2,0:T(8,128)S(1)}, f32[2,128,48]{1,2,0:T(8,128)S(1)}, u32[]{:S(2)}, u32[]{:S(2)}) collective-permute-start(f32[2,128,48]{1,2,0:T(8,128)S(1)} %get-tuple-element.975), channel_id=1, source_target_pairs={{120,0},{0,8},{8,16},{16,24},{24,32},{32,40},{40,48},{48,56},{56,6... | collective-permute-start | bytes 147464 | tf_op jit(solution)/shard_map/while/body/eval_jaxpr/ppermute | solution.py:15
  160.8 5.4 %collective-permute-start.1 = (bf16[2,128,48]{1,2,0:T(8,128)(2,1)S(1)}, bf16[2,128,48]{1,2,0:T(8,128)(2,1)S(1)}, u32[]{:S(2)}, u32[]{:S(2)}) collective-permute-start(bf16[2,128,48]{1,2,0:T(8,128)(2,1)S(1)} %get-tuple-element.976), channel_id=1, source_target_pairs={{120,0},{0,8},{8,16},{16,24},{24,32},{32,40},{40,48},{48,56},{56,6... | collective-permute-start | bytes 73736 | tf_op jit(solution)/shard_map/while/body/eval_jaxpr/ppermute | solution.py:15
  160.9 6.3 %collective-permute-start.2 = (f32[2,128,48]{1,2,0:T(8,128)S(1)}, f32[2,128,48]{1,2,0:T(8,128)S(1)}, u32[]{:S(2)}, u32[]{:S(2)}) collective-permute-start(f32[2,128,48]{1,2,0:T(8,128)S(1)} %get-tuple-element.975), channel_id=1, source_target_pairs={{120,0},{0,8},{8,16},{16,24},{24,32},{32,40},{40,48},{48,56},{56,6... | collective-permute-start | bytes 147464 | tf_op jit(solution)/shard_map/while/body/eval_jaxpr/ppermute | solution.py:15
  167.3 6.3 %collective-permute-start.2 = (f32[2,128,48]{1,2,0:T(8,128)S(1)}, f32[2,128,48]{1,2,0:T(8,128)S(1)}, u32[]{:S(2)}, u32[]{:S(2)}) collective-permute-start(f32[2,128,48]{1,2,0:T(8,128)S(1)} %get-tuple-element.975), channel_id=1, source_target_pairs={{120,0},{0,8},{8,16},{16,24},{24,32},{32,40},{40,48},{48,56},{56,6... | collective-permute-start | bytes 147464 | tf_op jit(solution)/shard_map/while/body/eval_jaxpr/ppermute | solution.py:15
  173.7 6.3 %collective-permute-start.2 = (f32[2,128,48]{1,2,0:T(8,128)S(1)}, f32[2,128,48]{1,2,0:T(8,128)S(1)}, u32[]{:S(2)}, u32[]{:S(2)}) collective-permute-start(f32[2,128,48]{1,2,0:T(8,128)S(1)} %get-tuple-element.975), channel_id=1, source_target_pairs={{120,0},{0,8},{8,16},{16,24},{24,32},{32,40},{40,48},{48,56},{56,6... | collective-permute-start | bytes 147464 | tf_op jit(solution)/shard_map/while/body/eval_jaxpr/ppermute | solution.py:15
  180.1 6.3 %collective-permute-start.2 = (f32[2,128,48]{1,2,0:T(8,128)S(1)}, f32[2,128,48]{1,2,0:T(8,128)S(1)}, u32[]{:S(2)}, u32[]{:S(2)}) collective-permute-start(f32[2,128,48]{1,2,0:T(8,128)S(1)} %get-tuple-element.975), channel_id=1, source_target_pairs={{120,0},{0,8},{8,16},{16,24},{24,32},{32,40},{40,48},{48,56},{56,6... | collective-permute-start | bytes 147464 | tf_op jit(solution)/shard_map/while/body/eval_jaxpr/ppermute | solution.py:15
  186.5 6.3 %collective-permute-start.2 = (f32[2,128,48]{1,2,0:T(8,128)S(1)}, f32[2,128,48]{1,2,0:T(8,128)S(1)}, u32[]{:S(2)}, u32[]{:S(2)}) collective-permute-start(f32[2,128,48]{1,2,0:T(8,128)S(1)} %get-tuple-element.975), channel_id=1, source_target_pairs={{120,0},{0,8},{8,16},{16,24},{24,32},{32,40},{40,48},{48,56},{56,6... | collective-permute-start | bytes 147464 | tf_op jit(solution)/shard_map/while/body/eval_jaxpr/ppermute | solution.py:15
  192.8 5.4 %collective-permute-start.1 = (bf16[2,128,48]{1,2,0:T(8,128)(2,1)S(1)}, bf16[2,128,48]{1,2,0:T(8,128)(2,1)S(1)}, u32[]{:S(2)}, u32[]{:S(2)}) collective-permute-start(bf16[2,128,48]{1,2,0:T(8,128)(2,1)S(1)} %get-tuple-element.976), channel_id=1, source_target_pairs={{120,0},{0,8},{8,16},{16,24},{24,32},{32,40},{40,48},{48,56},{56,6... | collective-permute-start | bytes 73736 | tf_op jit(solution)/shard_map/while/body/eval_jaxpr/ppermute | solution.py:15
  192.9 6.3 %collective-permute-start.2 = (f32[2,128,48]{1,2,0:T(8,128)S(1)}, f32[2,128,48]{1,2,0:T(8,128)S(1)}, u32[]{:S(2)}, u32[]{:S(2)}) collective-permute-start(f32[2,128,48]{1,2,0:T(8,128)S(1)} %get-tuple-element.975), channel_id=1, source_target_pairs={{120,0},{0,8},{8,16},{16,24},{24,32},{32,40},{40,48},{48,56},{56,6... | collective-permute-start | bytes 147464 | tf_op jit(solution)/shard_map/while/body/eval_jaxpr/ppermute | solution.py:15
  199.3 6.3 %collective-permute-start.2 = (f32[2,128,48]{1,2,0:T(8,128)S(1)}, f32[2,128,48]{1,2,0:T(8,128)S(1)}, u32[]{:S(2)}, u32[]{:S(2)}) collective-permute-start(f32[2,128,48]{1,2,0:T(8,128)S(1)} %get-tuple-element.975), channel_id=1, source_target_pairs={{120,0},{0,8},{8,16},{16,24},{24,32},{32,40},{40,48},{48,56},{56,6... | collective-permute-start | bytes 147464 | tf_op jit(solution)/shard_map/while/body/eval_jaxpr/ppermute | solution.py:15
  205.7 6.3 %collective-permute-start.2 = (f32[2,128,48]{1,2,0:T(8,128)S(1)}, f32[2,128,48]{1,2,0:T(8,128)S(1)}, u32[]{:S(2)}, u32[]{:S(2)}) collective-permute-start(f32[2,128,48]{1,2,0:T(8,128)S(1)} %get-tuple-element.975), channel_id=1, source_target_pairs={{120,0},{0,8},{8,16},{16,24},{24,32},{32,40},{40,48},{48,56},{56,6... | collective-permute-start | bytes 147464 | tf_op jit(solution)/shard_map/while/body/eval_jaxpr/ppermute | solution.py:15
  212.1 6.3 %collective-permute-start.2 = (f32[2,128,48]{1,2,0:T(8,128)S(1)}, f32[2,128,48]{1,2,0:T(8,128)S(1)}, u32[]{:S(2)}, u32[]{:S(2)}) collective-permute-start(f32[2,128,48]{1,2,0:T(8,128)S(1)} %get-tuple-element.975), channel_id=1, source_target_pairs={{120,0},{0,8},{8,16},{16,24},{24,32},{32,40},{40,48},{48,56},{56,6... | collective-permute-start | bytes 147464 | tf_op jit(solution)/shard_map/while/body/eval_jaxpr/ppermute | solution.py:15
  218.4 6.3 %collective-permute-start.2 = (f32[2,128,48]{1,2,0:T(8,128)S(1)}, f32[2,128,48]{1,2,0:T(8,128)S(1)}, u32[]{:S(2)}, u32[]{:S(2)}) collective-permute-start(f32[2,128,48]{1,2,0:T(8,128)S(1)} %get-tuple-element.975), channel_id=1, source_target_pairs={{120,0},{0,8},{8,16},{16,24},{24,32},{32,40},{40,48},{48,56},{56,6... | collective-permute-start | bytes 147464 | tf_op jit(solution)/shard_map/while/body/eval_jaxpr/ppermute | solution.py:15
  224.8 6.3 %collective-permute-start.2 = (f32[2,128,48]{1,2,0:T(8,128)S(1)}, f32[2,128,48]{1,2,0:T(8,128)S(1)}, u32[]{:S(2)}, u32[]{:S(2)}) collective-permute-start(f32[2,128,48]{1,2,0:T(8,128)S(1)} %get-tuple-element.975), channel_id=1, source_target_pairs={{120,0},{0,8},{8,16},{16,24},{24,32},{32,40},{40,48},{48,56},{56,6... | collective-permute-start | bytes 147464 | tf_op jit(solution)/shard_map/while/body/eval_jaxpr/ppermute | solution.py:15
  231.2 6.3 %collective-permute-start.2 = (f32[2,128,48]{1,2,0:T(8,128)S(1)}, f32[2,128,48]{1,2,0:T(8,128)S(1)}, u32[]{:S(2)}, u32[]{:S(2)}) collective-permute-start(f32[2,128,48]{1,2,0:T(8,128)S(1)} %get-tuple-element.975), channel_id=1, source_target_pairs={{120,0},{0,8},{8,16},{16,24},{24,32},{32,40},{40,48},{48,56},{56,6... | collective-permute-start | bytes 147464 | tf_op jit(solution)/shard_map/while/body/eval_jaxpr/ppermute | solution.py:15
  239.5 14.7 %all-to-all-start.1 = ((bf16[2,128,2048]{1,0,2:T(2,128)(2,1)}), bf16[2,128,2048]{1,0,2:T(2,128)(2,1)S(1)}, u32[]{:S(2)}, u32[]{:S(2)}) async-start(bf16[2,128,2048]{1,0,2:T(2,128)(2,1)} %copy.45), calls=%async_computation.1 | async-start | bytes 2097152 | tf_op jit(solution)/shard_map/all_to_all | solution.py:170
  243.4 5.7 %collective-permute-start.3 = (bf16[2,128,48]{1,2,0:T(8,128)(2,1)S(1)}, bf16[2,128,48]{1,2,0:T(8,128)(2,1)S(1)}, u32[]{:S(2)}, u32[]{:S(2)}) collective-permute-start(bf16[2,128,48]{1,2,0:T(8,128)(2,1)S(1)} %convert.12), channel_id=1, source_target_pairs={{120,0},{0,8},{8,16},{16,24},{24,32},{32,40},{40,48},{48,56},{56,6... | collective-permute-start | bytes 73736 | tf_op jit(solution)/shard_map/ppermute | solution.py:15
  (35 other events, 443.2 us)
where the time goes:
time: 365 us; the launch traced here: 364 us
  waiting for transfers between devices  137 us (38%)
  blocking collectives  71.2 us (20%)
  local copies, waits for them, and re-layouts  59.1 us (16%)
  matrix products  44.5 us (12%)
  other arithmetic  24.2 us (7%)
  starting transfers between devices  23.1 us (6%)
    ppermute x46, waiting for transfers between devices, from_behind(): return lax.ppermute(block, axis, route)  120 us
    psum x1, blocking collectives, local(): grad_weight, grad_gain = lax.psum((weight_part, gain_part), ('blk', 'col'))  71.2 us
    unnamed x25, local copies, waits for them, and re-layouts  23.9 us
    dynamic_slice x30, local copies, waits for them, and re-layouts, tile_allowed(): chain_cols = lax.dynamic_slice_in_dim(chain_ids, col_start, count)  22.9 us
    all_to_all x1, waiting for transfers between devices, local(): lax.all_to_all(bias_local, 'col', split_axis=0, concat_axis=2, tiled=True)  12.8 us
    ppermute x46, starting transfers between devices, from_behind(): return lax.ppermute(block, axis, route)  11 us
    dot_general x1, matrix products, local(): jnp.einsum('hij,ch->ijc', dbias_cells, bias_weight, preferred_element_typ...  8.87 us
    convert_element_type x1, other arithmetic, local(): grad_pair = (inverse * (scaled - jnp.mean(scaled, axis=-1, keepdims=True)...  8.53 us
  transfers between devices with their start and end apart: 48, of which 32 were waited for; matrix products, arithmetic and copies ran while one was open for 14% of the time, Pallas kernels for 0%

commit v1 on v0

v1 whole, which is shorter than its diff:
```python
import math

import jax
import jax.numpy as jnp
from jax import lax
from jax.sharding import PartitionSpec as P

HEAD_DIM = 24
MASK_BLOCK = 128


def pair_norm(pair_rows, norm_gain):
    values = pair_rows.astype(jnp.float32)
    centre = jnp.mean(values, axis=-1, keepdims=True)
    shifted = values - centre
    inverse = lax.rsqrt(jnp.mean(shifted * shifted, axis=-1, keepdims=True) + 1e-05)
    unit = shifted * inverse
    normed = (unit * norm_gain).astype(jnp.bfloat16)
    return (unit, inverse, normed)


def block_onehot(first_token, count, nblocks):
    block_ids = (first_token + jnp.arange(count, dtype=jnp.int32)) // MASK_BLOCK
    return (block_ids[:, None] == jnp.arange(nblocks, dtype=jnp.int32)[None, :]).astype(
        jnp.bfloat16
    )


def local(
    queries, key_proj, value_proj, out_grad, pair_rep, norm_gain, bias_weight, chain_ids, block_mask
):
    tok_rows = queries.shape[0]
    local_width = queries.shape[1]
    local_heads = local_width // HEAD_DIM
    scale_factor = 1.0 / math.sqrt(HEAD_DIM)
    blk_index = lax.axis_index("blk")
    blk_count = lax.axis_size("blk")
    all_tokens = blk_count * tok_rows
    row_start = blk_index * tok_rows
    nblocks = block_mask.shape[0]
    rows_table = jnp.dot(
        block_onehot(row_start, tok_rows, nblocks),
        block_mask.astype(jnp.bfloat16),
        preferred_element_type=jnp.float32,
    ).astype(jnp.bfloat16)
    chain_rows = lax.dynamic_slice_in_dim(chain_ids, row_start, tok_rows)
    hits = lax.dot_general(
        rows_table,
        block_onehot(0, all_tokens, nblocks),
        (((1,), (1,)), ((), ())),
        preferred_element_type=jnp.float32,
    )
    allowed = (hits > 0.5) | (chain_rows[:, None] == chain_ids[None, :])

    unit, inverse, normed = pair_norm(pair_rep, norm_gain)
    kv_local = jnp.stack([key_proj, value_proj])
    kv_all = lax.all_gather(kv_local, "blk", axis=1, tiled=True)
    query_heads = queries.reshape(tok_rows, local_heads, HEAD_DIM)
    grad_heads = out_grad.reshape(tok_rows, local_heads, HEAD_DIM)
    key_heads = kv_all[0].reshape(all_tokens, local_heads, HEAD_DIM)
    value_heads = kv_all[1].reshape(all_tokens, local_heads, HEAD_DIM)
    bias_local = jnp.einsum(
        "ijc,ch->hij", normed, bias_weight, preferred_element_type=jnp.float32
    ).astype(jnp.bfloat16)
    bias_mine = lax.all_to_all(bias_local, "col", split_axis=0, concat_axis=2, tiled=True)

    scores = (
        jnp.einsum("qhd,khd->hqk", query_heads, key_heads, preferred_element_type=jnp.float32)
        * scale_factor
        + bias_mine.astype(jnp.float32)
    )
    masked = jnp.where(allowed[None], scores, -jnp.inf)
    row_top = jnp.max(masked, axis=-1, keepdims=True)
    expo = jnp.where(allowed[None], jnp.exp(scores - row_top), 0.0)
    totals = jnp.sum(expo, axis=-1, keepdims=True)
    log_total = row_top + jnp.log(totals)
    weights = jnp.where(allowed[None], jnp.exp(scores - log_total), 0.0)
    probs = weights.astype(jnp.bfloat16)
    attended = jnp.einsum("hqk,khd->qhd", weights, value_heads.astype(jnp.float32))
    delta = jnp.sum(grad_heads.astype(jnp.float32) * attended, axis=-1).T
    dprobs = jnp.einsum(
        "qhd,khd->hqk", grad_heads, value_heads, preferred_element_type=jnp.float32
    )
    dscores = (probs.astype(jnp.float32) * (dprobs - delta[:, :, None])).astype(jnp.bfloat16)
    query_add = (
        jnp.einsum("hqk,khd->qhd", dscores, key_heads, preferred_element_type=jnp.float32)
        * scale_factor
    )
    key_add = (
        jnp.einsum("hqk,qhd->khd", dscores, query_heads, preferred_element_type=jnp.float32)
        * scale_factor
    )
    value_add = jnp.einsum("hqk,qhd->khd", probs, grad_heads, preferred_element_type=jnp.float32)
    kv_part = jnp.stack(
        [key_add.reshape(all_tokens, local_width), value_add.reshape(all_tokens, local_width)]
    )
    kv_grads = lax.psum_scatter(kv_part, "blk", scatter_dimension=1, tiled=True)
    grad_queries = query_add.reshape(tok_rows, local_width).astype(jnp.bfloat16)
    grad_keys = kv_grads[0].astype(jnp.bfloat16)
    grad_values = kv_grads[1].astype(jnp.bfloat16)
    dbias_cells = lax.all_to_all(dscores, "col", split_axis=2, concat_axis=0, tiled=True)
    dnormed = jnp.einsum(
        "hij,ch->ijc", dbias_cells, bias_weight, preferred_element_type=jnp.float32
    )
    gain_part = jnp.sum(dnormed * unit, axis=(0, 1))
    weight_part = jnp.einsum("ijc,hij->ch", normed, dbias_cells, preferred_element_type=jnp.float32)
    pair_width = gain_part.shape[0]
    packed = jnp.concatenate([gain_part, weight_part.reshape(-1)])
    packed = lax.psum(packed, ("blk", "col"))
    grad_gain = packed[:pair_width]
    grad_weight = packed[pair_width:].reshape(weight_part.shape)
    scaled = dnormed * norm_gain
    grad_pair = (
        inverse
        * (
            scaled
            - jnp.mean(scaled, axis=-1, keepdims=True)
            - unit * jnp.mean(scaled * unit, axis=-1, keepdims=True)
        )
    ).astype(jnp.bfloat16)
    return (grad_queries, grad_keys, grad_values, grad_pair, grad_gain, grad_weight)


def solution(mesh):
    placed = (
        P("blk", "col"),
        P("blk", "col"),
        P("blk", "col"),
        P("blk", "col"),
        P("blk", "col", None),
        P(),
        P(),
        P(),
        P(),
    )
    return jax.shard_map(
        local,
        mesh=mesh,
        in_specs=placed,
        out_specs=(
            P("blk", "col"),
            P("blk", "col"),
            P("blk", "col"),
            P("blk", "col", None),
            P(),
            P(),
        ),
        check_vma=False,
    )
```

time: 365 us -> 233 us (0.64)
  waiting for transfers between devices: 137 us -> 9.72 us
  blocking collectives: 71.2 us -> 91.3 us
  local copies, waits for them, and re-layouts: 59.1 us -> 44.3 us
  matrix products: 44.5 us -> 31.1 us
  between operations: 1 us -> 14.3 us
  starting transfers between devices: 23.1 us -> 15.2 us
    ppermute x46 -> x0, waiting for transfers between devices: 120 us -> none  [from_behind(): return lax.ppermute(block, axis, route)]
    all_gather x0 -> x1, blocking collectives: none -> 26.3 us  [local(): kv_all = lax.all_gather(kv_local, 'blk', axis=1, tiled=True)]
    dynamic_slice x60 -> x0, local copies, waits for them, and re-layouts: 25 us -> none  [the longest x30 22.9 us: tile_allowed(): chain_cols = lax.dynamic_slice_in_dim(chain_ids, col_start, count)]
    dot_general x143 -> x7, matrix products: 26.8 us -> 10.2 us  [the longest x1 2.43 us: local(): jnp.einsum('qhd,khd->hqk', query_heads, key_heads, preferred_element_type...]
    all_to_all x1, waiting for transfers between devices: 12.8 us -> 0.01 us  [local(): lax.all_to_all(bias_local, 'col', split_axis=0, concat_axis=2, tiled=True)]
    convert_element_type x1 -> x2, local copies, waits for them, and re-layouts: 0.13 us -> 11.1 us  [the longest x1 9.48 us: local(): (probs.astype(jnp.float32) * (dprobs - delta[:, :, None])).astype(jnp.bfl...]
    ppermute x46 -> x0, starting transfers between devices: 11 us -> none  [from_behind(): return lax.ppermute(block, axis, route)]
    psum x1, blocking collectives: 71.2 us -> 65.1 us  [local(): packed = lax.psum(packed, ('blk', 'col'))]
  transfers between devices with their start and end apart: 48 -> 3, of which waited for: 32 -> 1; matrix products, arithmetic and copies ran while one was open for 14% -> 24% of each run, Pallas kernels for 0% -> 0%
where the time goes in v1:
time: 233 us; the launch traced here: 232 us
  blocking collectives  91.3 us (39%)
  local copies, waits for them, and re-layouts  44.3 us (19%)
  matrix products  31.1 us (13%)
  other arithmetic  26 us (11%)
  starting transfers between devices  15.2 us (7%)
  between operations  14.3 us (6%)
  waiting for transfers between devices  9.72 us (4%)
    psum x1, blocking collectives, local(): packed = lax.psum(packed, ('blk', 'col'))  65.1 us
    all_gather x1, blocking collectives, local(): kv_all = lax.all_gather(kv_local, 'blk', axis=1, tiled=True)  26.3 us
    unnamed x31, local copies, waits for them, and re-layouts  24.6 us
    convert_element_type x1, other arithmetic, local(): grad_pair = (inverse * (scaled - jnp.mean(scaled, axis=-1, keepdims=True)...  13.6 us
    dot_general x1, matrix products, local(): jnp.einsum('hij,ch->ijc', dbias_cells, bias_weight, preferred_element_typ...  12.2 us
    all_to_all x1, waiting for transfers between devices, local(): lax.all_to_all(dscores, 'col', split_axis=2, concat_axis=0, tiled=True)  9.7 us
    convert_element_type x1, local copies, waits for them, and re-layouts, local(): (probs.astype(jnp.float32) * (dprobs - delta[:, :, None])).astype(jnp.bfl...  9.48 us
    all_to_all x1, starting transfers between devices, local(): lax.all_to_all(bias_local, 'col', split_axis=0, concat_axis=2, tiled=True)  8.31 us
  transfers between devices with their start and end apart: 3, of which 1 were waited for; matrix products, arithmetic and copies ran while one was open for 24% of the time, Pallas kernels for 0%

profile of v1, /device:TPU:1, one launch (start us, length us, event | category | flops | bytes accessed | tf_op | source)
XLA Modules:
  0.0 232.0 jit_solution(2193605307160610301)
XLA Ops:
  7.2 11.9 %copy.40 = bf16[128,256,128]{1,2,0:T(8,128)(2,1)} copy(bf16[128,256,128]{2,1,0:T(8,128)(2,1)} %param.13) | data formatting | bytes 16777216 | tf_op args[4]
  19.1 6.1 %convert_reduce_fusion = f32[128,256]{1,0:T(8,128)S(1)} fusion(bf16[128,256,128]{1,2,0:T(8,128)(2,1)} %copy.40), kind=kLoop, calls=%fused_computation.1 | loop fusion | flops 8355840 | bytes 8519680 | tf_op jit(solution)/shard_map/reduce_sum | solution.py:14
  25.2 4.0 %fusion.12 = f32[128,256]{1,0:T(8,128)S(1)} fusion(bf16[128,256,128]{1,2,0:T(8,128)(2,1)S(1)} %copy-done.2, f32[128,256]{1,0:T(8,128)S(1)} %broadcast_multiply_fusion.2), kind=kLoop, calls=%fused_computation.14 | loop fusion | flops 16744448 | bytes 8650752 | tf_op jit(solution)/shard_map/reduce_sum | solution.py:16
  29.3 2.6 %fusion.21 = bf16[16,128,256]{2,0,1:T(8,128)(2,1)S(1)} fusion(bf16[128,256,128]{1,2,0:T(8,128)(2,1)S(1)} %copy-done.2, f32[128]{0:T(128)S(1)} %copy-done.8, f32[128,256]{1,0:T(8,128)S(1)} %add_rsqrt_fusion, f32[128,256]{1,0:T(8,128)S(1)} %broadcast_multiply_fusion.2, bf16[128,16]{0,1:T(8,128)(2,1)S(1)} %copy-done.12), kind=kOutput, calls=%fused_computation.32 | convolution fusion | flops 155713536 | bytes 9703936 | tf_op jit(solution)/shard_map/ijc,ch->hij/dot_general | solution.py:62
  31.9 1.4 copy.42
  33.2 8.3 %all-to-all-start = ((bf16[16,128,256]{2,1,0:T(8,128)(2,1)}), bf16[16,128,256]{2,1,0:T(8,128)(2,1)S(1)}, u32[]{:S(2)}, u32[]{:S(2)}) async-start(bf16[16,128,256]{2,1,0:T(8,128)(2,1)} %copy.42), calls=%async_computation | async-start | bytes 2097152 | tf_op jit(solution)/shard_map/all_to_all | solution.py:65
  41.7 0.8 fusion.18
  43.0 26.3 %all_gather.3 = bf16[2,2048,48]{1,2,0:T(8,128)(2,1)S(1)} all-gather(bf16[2,128,48]{1,2,0:T(8,128)(2,1)S(1)} %pad_maximum_fusion.1), channel_id=1, replica_groups=mesh['blk'=16,'col'=8] {'blk'}, dimensions={1}, use_global_device_ids=true | all-gather | bytes 417792 | tf_op jit(solution)/shard_map/all_gather | solution.py:57
  70.0 1.6 copy.43
  71.7 2.4 %select_reduce_fusion.1 = (f32[2,128]{1,0:T(2,128)S(1)}, f32[2,128,2048]{1,2,0:T(8,128)S(1)}) fusion(pred[128,2048]{0,1:T(8,128)(4,1)S(1)} %copy.39, f32[2,128,2048]{1,2,0:T(8,128)} %bitcast.70, bf16[2048,2,24]{0,2,1:T(8,128)(2,1)} %bitcast.73, bf16[128,2,24]{0,2,1:T(8,128)(2,1)S(1)} %bitcast.68), kind=kOutput, calls=%fused_computation.28 | convolution fusion | flops 27262720 | bytes 4666368 | tf_op jit(solution)/shard_map/qhd,khd->hqk/dot_general | solution.py:68
  74.6 1.5 fusion.31
  76.1 1.6 fusion.17
  77.7 9.5 %copy.48 = bf16[2,128,2048]{1,0,2:T(2,128)(2,1)} copy(bf16[2,128,2048]{1,2,0:T(8,128)(2,1)S(1)} %fusion.17) | data formatting | bytes 2097152 | tf_op jit(solution)/shard_map/convert_element_type | solution.py:84
  87.1 6.6 %all-to-all-start.1 = ((bf16[2,128,2048]{1,0,2:T(2,128)(2,1)}), bf16[2,128,2048]{1,0,2:T(2,128)(2,1)}, u32[]{:S(2)}, u32[]{:S(2)}) async-start(bf16[2,128,2048]{1,0,2:T(2,128)(2,1)} %copy.48), calls=%async_computation.2 | async-start | bytes 2097152 | tf_op jit(solution)/shard_map/all_to_all | solution.py:101
  94.7 1.4 fusion.38
  96.1 1.0 pad_maximum_fusion
  97.1 1.8 fusion.30
  98.9 9.7 %all-to-all-done.1 = bf16[2,128,2048]{1,0,2:T(2,128)(2,1)} async-done(((bf16[2,128,2048]{1,0,2:T(2,128)(2,1)}), bf16[2,128,2048]{1,0,2:T(2,128)(2,1)}, u32[]{:S(2)}, u32[]{:S(2)}) %all-to-all-start.1) | async-done | bytes 1048608 | tf_op jit(solution)/shard_map/all_to_all | solution.py:101
  108.6 4.2 %copy.49 = bf16[2,128,8,256]{3,0,2,1:T(2,128)(2,1)S(1)} copy(bf16[2,128,8,256]{1,0,3,2:T(2,128)(2,1)} %bitcast.23) | data formatting | bytes 2097152 | tf_op jit(solution)/shard_map/all_to_all | solution.py:101
  113.3 6.1 %fusion.25 = f32[128,16]{1,0:T(8,128)S(1)} fusion(bf16[16,128,256]{2,0,1:T(8,128)(2,1)S(1)} %all_to_all.24, bf16[128,256,128]{1,2,0:T(8,128)(2,1)} %copy.40, f32[128]{0:T(128)} %param.14, f32[128,256]{1,0:T(8,128)} %copy-done.3, f32[128,256]{1,0:T(8,128)S(1)} %broadcast_multiply_fusion.2), kind=kOutput, calls=%fused_computation.34 | convolution fusion | flops 155189248 | bytes 9708032 | tf_op jit(solution)/shard_map/ijc,hij->ch/dot_general | solution.py:106
  119.4 12.2 %fusion.11 = (f32[128]{0:T(128)S(1)}, f32[128,256]{1,0:T(8,128)S(1)}, f32[128,256]{1,0:T(8,128)S(1)}, f32[128,256,128]{1,2,0:T(8,128)}) fusion(bf16[128,256,128]{1,2,0:T(8,128)(2,1)} %copy.40, f32[128,256]{1,0:T(8,128)S(1)} %copy-done.4, f32[128,256]{1,0:T(8,128)S(1)} %broadcast_multiply_fusion.2, f32[128]{0:T(128)S(1)} %copy-done.9, ...), kind=kOutput, calls=%fused_computation.13 | convolution fusion | flops 171900800 | bytes 26743808 | tf_op jit(solution)/shard_map/hij,ch->ijc/dot_general | solution.py:102
  131.8 65.1 %psum.7 = f32[2176]{0:T(1024)S(1)} all-reduce(f32[2176]{0:T(1024)S(1)} %pad_maximum_fusion.2), channel_id=1, replica_groups=mesh['blk'=16,'col'=8] {'blk','col'}, use_global_device_ids=true, to_apply=%region_9.10 | all-reduce | flops 2176 | bytes 17408 | tf_op jit(solution)/shard_map/psum | solution.py:109
  198.1 13.6 %fusion.10 = bf16[128,256,128]{1,2,0:T(8,128)(2,1)} fusion(bf16[128,256,128]{1,2,0:T(8,128)(2,1)} %copy.40, f32[128,256,128]{1,2,0:T(8,128)} %get-tuple-element.33, f32[128,256]{1,0:T(8,128)S(1)} %get-tuple-element.34, f32[128,256]{1,0:T(8,128)S(1)} %get-tuple-element.35, f32[128]{0:T(128)S(1)} %copy-done.9, f32[128,256]{1,0:T(8,128)S(1)} %copy-done.4, ...), kind=kLoop, calls=%fused_computation.12 | loop fusion | flops 37748736 | bytes 34079232 | tf_op jit(solution)/shard_map/convert_element_type | solution.py:120
  211.8 11.9 %copy.52 = bf16[128,256,128]{2,1,0:T(8,128)(2,1)} copy(bf16[128,256,128]{1,2,0:T(8,128)(2,1)} %fusion.10) | data formatting | bytes 16777216
  (53 shorter events, 6.0 us)
Async XLA Ops:
  7.2 64.5 %copy-start = (bf16[128,48]{0,1:T(8,128)(2,1)S(1)}, bf16[128,48]{0,1:T(8,128)(2,1)}, u32[]{:S(2)}) copy-start(bf16[128,48]{0,1:T(8,128)(2,1)} %param.9) | copy-start | bytes 36868
  19.1 6.1 %copy-start.2 = (bf16[128,256,128]{1,2,0:T(8,128)(2,1)S(1)}, bf16[128,256,128]{1,2,0:T(8,128)(2,1)}, u32[]{:S(2)}) copy-start(bf16[128,256,128]{1,2,0:T(8,128)(2,1)} %copy.40) | copy-start | bytes 25165828
  19.1 10.1 %copy-start.8 = (f32[128]{0:T(128)S(1)}, f32[128]{0:T(128)}, u32[]{:S(2)}) copy-start(f32[128]{0:T(128)} %param.14) | copy-start | bytes 1540
  19.1 10.1 %copy-start.12 = (bf16[128,16]{0,1:T(8,128)(2,1)S(1)}, bf16[128,16]{0,1:T(8,128)(2,1)}, u32[]{:S(2)}) copy-start(bf16[128,16]{0,1:T(8,128)(2,1)} %param.15) | copy-start | bytes 12292
  29.2 2.7 %copy-start.3 = (f32[128,256]{1,0:T(8,128)}, f32[128,256]{1,0:T(8,128)S(1)}, u32[]{:S(2)}) copy-start(f32[128,256]{1,0:T(8,128)S(1)} %add_rsqrt_fusion) | copy-start | bytes 393220
  29.2 12.4 %copy-start.10 = (s32[2048]{0:T(1024)S(1)}, s32[2048]{0:T(1024)}, u32[]{:S(2)}) copy-start(s32[2048]{0:T(1024)} %param.16) | copy-start | bytes 24580
  29.2 12.4 %copy-start.11 = (s32[16,16]{1,0:T(8,128)S(1)}, s32[16,16]{1,0:T(8,128)}, u32[]{:S(2)}) copy-start(s32[16,16]{1,0:T(8,128)} %param.17) | copy-start | bytes 3076
  29.3 13.7 %copy-start.6 = (bf16[128,48]{0,1:T(8,128)(2,1)S(1)}, bf16[128,48]{0,1:T(8,128)(2,1)}, u32[]{:S(2)}) copy-start(bf16[128,48]{0,1:T(8,128)(2,1)} %param.11) | copy-start | bytes 36868
  29.3 13.7 %copy-start.7 = (bf16[128,48]{0,1:T(8,128)(2,1)S(1)}, bf16[128,48]{0,1:T(8,128)(2,1)}, u32[]{:S(2)}) copy-start(bf16[128,48]{0,1:T(8,128)(2,1)} %param.10) | copy-start | bytes 36868
  33.2 36.8 %all-to-all-start = ((bf16[16,128,256]{2,1,0:T(8,128)(2,1)}), bf16[16,128,256]{2,1,0:T(8,128)(2,1)S(1)}, u32[]{:S(2)}, u32[]{:S(2)}) async-start(bf16[16,128,256]{2,1,0:T(8,128)(2,1)} %copy.42), calls=%async_computation | async-start | bytes 2097152 | tf_op jit(solution)/shard_map/all_to_all | solution.py:65
  71.7 4.4 %copy-start.5 = (bf16[1,2048,48]{1,2,0:T(8,128)(2,1)S(1)}, bf16[1,2048,48]{1,2,0:T(8,128)(2,1)}, u32[]{:S(2)}) copy-start(bf16[1,2048,48]{1,2,0:T(8,128)(2,1)} %get-tuple-element.27) | copy-start | bytes 589828
  87.1 21.5 %all-to-all-start.1 = ((bf16[2,128,2048]{1,0,2:T(2,128)(2,1)}), bf16[2,128,2048]{1,0,2:T(2,128)(2,1)}, u32[]{:S(2)}, u32[]{:S(2)}) async-start(bf16[2,128,2048]{1,0,2:T(2,128)(2,1)} %copy.48), calls=%async_computation.2 | async-start | bytes 2097152 | tf_op jit(solution)/shard_map/all_to_all | solution.py:101
  93.8 129.9 %reduce-scatter.2.cloned.1.call-start = ((), (), s32[]{:S(2)}) async-start(), calls=%async_computation.3 | async-start | bytes 835584 | tf_op jit(solution)/shard_map/reduce_scatter | solution.py:97
  113.3 6.1 %copy-start.4 = (f32[128,256]{1,0:T(8,128)S(1)}, f32[128,256]{1,0:T(8,128)}, u32[]{:S(2)}) copy-start(f32[128,256]{1,0:T(8,128)} %copy-done.3) | copy-start | bytes 393220
  113.3 6.1 %copy-start.9 = (f32[128]{0:T(128)S(1)}, f32[128]{0:T(128)}, u32[]{:S(2)}) copy-start(f32[128]{0:T(128)} %param.14) | copy-start | bytes 1540
  113.3 6.1 %copy-start.13 = (bf16[128,16]{0,1:T(8,128)(2,1)S(1)}, bf16[128,16]{0,1:T(8,128)(2,1)}, u32[]{:S(2)}) copy-start(bf16[128,16]{0,1:T(8,128)(2,1)} %param.15) | copy-start | bytes 12292
  198.1 27.0 %copy-start.1 = (bf16[128,48]{0,1:T(8,128)(2,1)S(1)}, bf16[128,48]{0,1:T(8,128)(2,1)}, u32[]{:S(2)}) copy-start(bf16[128,48]{0,1:T(8,128)(2,1)} %param.9) | copy-start | bytes 36868
Sparse Core Ops, SparseCore 0:
  97.2 58.6 reduce-scatter.1

commit v2 on v1

--- a/solution.py
+++ b/solution.py
@@ -54,7 +54,9 @@
 
     unit, inverse, normed = pair_norm(pair_rep, norm_gain)
     kv_local = jnp.stack([key_proj, value_proj])
-    kv_all = lax.all_gather(kv_local, "blk", axis=1, tiled=True)
+    kv_rep = jnp.broadcast_to(kv_local[None], (blk_count,) + kv_local.shape)
+    kv_all = lax.all_to_all(kv_rep, "blk", split_axis=0, concat_axis=0, tiled=True)
+    kv_all = jnp.transpose(kv_all, (1, 0, 2, 3)).reshape(2, all_tokens, local_width)
     query_heads = queries.reshape(tok_rows, local_heads, HEAD_DIM)
     grad_heads = out_grad.reshape(tok_rows, local_heads, HEAD_DIM)
     key_heads = kv_all[0].reshape(all_tokens, local_heads, HEAD_DIM)
@@ -106,7 +108,7 @@
     weight_part = jnp.einsum("ijc,hij->ch", normed, dbias_cells, preferred_element_type=jnp.float32)
     pair_width = gain_part.shape[0]
     packed = jnp.concatenate([gain_part, weight_part.reshape(-1)])
-    packed = lax.psum(packed, ("blk", "col"))
+    packed = jnp.sum(lax.all_gather(lax.psum(packed, "col"), "blk"), axis=0)
     grad_gain = packed[:pair_width]
     grad_weight = packed[pair_width:].reshape(weight_part.shape)
     scaled = dnormed * norm_gain

time: 233 us -> 204 us (0.88)
  blocking collectives: 91.3 us -> 43.9 us
  waiting for transfers between devices: 9.72 us -> 21.1 us
  starting transfers between devices: 15.2 us -> 19.7 us
    psum x1, blocking collectives: 65.1 us -> 20.4 us  [local(): packed = jnp.sum(lax.all_gather(lax.psum(packed, 'col'), 'blk'), axis=0)]
    all_to_all x1, waiting for transfers between devices: 0.01 us -> 11.7 us  [local(): lax.all_to_all(bias_local, 'col', split_axis=0, concat_axis=2, tiled=True)]
    all_to_all x0 -> x1, starting transfers between devices: none -> 6.9 us  [local(): lax.all_to_all(kv_rep, 'blk', split_axis=0, concat_axis=0, tiled=True)]
    all_gather x1, blocking collectives: 26.3 us -> 23.5 us  [local(): packed = jnp.sum(lax.all_gather(lax.psum(packed, 'col'), 'blk'), axis=0)]
    unnamed x31 -> x27, local copies, waits for them, and re-layouts: 24.6 us -> 24.6 us
  transfers between devices with their start and end apart: 3 -> 4, of which waited for: 1 -> 2; matrix products, arithmetic and copies ran while one was open for 24% -> 41% of each run, Pallas kernels for 0% -> 0%
where the time goes in v2:
time: 204 us; the launch traced here: 203 us
  local copies, waits for them, and re-layouts  45.9 us (22%)
  blocking collectives  43.9 us (22%)
  matrix products  31.2 us (15%)
  other arithmetic  26.8 us (13%)
  waiting for transfers between devices  21.1 us (10%)
  starting transfers between devices  19.7 us (10%)
  between operations  14.3 us (7%)
    unnamed x27, local copies, waits for them, and re-layouts  24.6 us
    all_gather x1, blocking collectives, local(): packed = jnp.sum(lax.all_gather(lax.psum(packed, 'col'), 'blk'), axis=0)  23.5 us
    psum x1, blocking collectives, local(): packed = jnp.sum(lax.all_gather(lax.psum(packed, 'col'), 'blk'), axis=0)  20.4 us
    convert_element_type x1, other arithmetic, local(): grad_pair = (inverse * (scaled - jnp.mean(scaled, axis=-1, keepdims=True)...  13.7 us
    dot_general x1, matrix products, local(): jnp.einsum('hij,ch->ijc', dbias_cells, bias_weight, preferred_element_typ...  12.2 us
    all_to_all x1, waiting for transfers between devices, local(): lax.all_to_all(bias_local, 'col', split_axis=0, concat_axis=2, tiled=True)  11.7 us
    convert_element_type x1, local copies, waits for them, and re-layouts, local(): (probs.astype(jnp.float32) * (dprobs - delta[:, :, None])).astype(jnp.bfl...  9.48 us
    all_to_all x1, waiting for transfers between devices, local(): lax.all_to_all(dscores, 'col', split_axis=2, concat_axis=0, tiled=True)  9.38 us
  transfers between devices with their start and end apart: 4, of which 2 were waited for; matrix products, arithmetic and copies ran while one was open for 41% of the time, Pallas kernels for 0%

profile of v2, /device:TPU:1, one launch (start us, length us, event | category | flops | bytes accessed | tf_op | source)
XLA Modules:
  0.0 202.9 jit_solution(3818930280727681458)
XLA Ops:
  8.7 6.9 %all-to-all-start = ((bf16[16,2,128,48]{2,3,1,0:T(8,128)(2,1)}), bf16[16,2,128,48]{2,3,1,0:T(8,128)(2,1)S(1)}, u32[]{:S(2)}, u32[]{:S(2)}) async-start(bf16[16,2,128,48]{2,3,1,0:T(8,128)(2,1)} %broadcast_in_dim.24), calls=%async_computation | async-start | bytes 786432 | tf_op jit(solution)/shard_map/all_to_all | solution.py:58
  15.6 11.9 %copy.41 = bf16[128,256,128]{1,2,0:T(8,128)(2,1)} copy(bf16[128,256,128]{2,1,0:T(8,128)(2,1)} %param.13) | data formatting | bytes 16777216 | tf_op args[4]
  27.5 6.1 %convert_reduce_fusion = f32[128,256]{1,0:T(8,128)S(1)} fusion(bf16[128,256,128]{1,2,0:T(8,128)(2,1)} %copy.41), kind=kLoop, calls=%fused_computation.1 | loop fusion | flops 8355840 | bytes 8519680 | tf_op jit(solution)/shard_map/reduce_sum | solution.py:14
  33.6 4.0 %fusion.12 = f32[128,256]{1,0:T(8,128)S(1)} fusion(bf16[128,256,128]{1,2,0:T(8,128)(2,1)S(1)} %copy-done.2, f32[128,256]{1,0:T(8,128)S(1)} %broadcast_multiply_fusion.2), kind=kLoop, calls=%fused_computation.14 | loop fusion | flops 16744448 | bytes 8650752 | tf_op jit(solution)/shard_map/reduce_sum | solution.py:16
  37.7 2.6 %fusion.21 = bf16[16,128,256]{2,0,1:T(8,128)(2,1)S(1)} fusion(bf16[128,256,128]{1,2,0:T(8,128)(2,1)S(1)} %copy-done.2, f32[128]{0:T(128)S(1)} %copy-done.6, f32[128,256]{1,0:T(8,128)S(1)} %add_rsqrt_fusion, f32[128,256]{1,0:T(8,128)S(1)} %broadcast_multiply_fusion.2, bf16[128,16]{0,1:T(8,128)(2,1)S(1)} %copy-done.10), kind=kOutput, calls=%fused_computation.32 | convolution fusion | flops 155713536 | bytes 9703936 | tf_op jit(solution)/shard_map/ijc,ch->hij/dot_general | solution.py:64
  40.3 1.4 copy.43
  41.7 7.2 %all-to-all-start.1 = ((bf16[16,128,256]{2,1,0:T(8,128)(2,1)}), bf16[16,128,256]{2,1,0:T(8,128)(2,1)S(1)}, u32[]{:S(2)}, u32[]{:S(2)}) async-start(bf16[16,128,256]{2,1,0:T(8,128)(2,1)} %copy.43), calls=%async_computation.1 | async-start | bytes 2097152 | tf_op jit(solution)/shard_map/all_to_all | solution.py:67
  52.0 11.7 %all-to-all-done.1 = bf16[16,128,256]{2,1,0:T(8,128)(2,1)S(1)} async-done(((bf16[16,128,256]{2,1,0:T(8,128)(2,1)}), bf16[16,128,256]{2,1,0:T(8,128)(2,1)S(1)}, u32[]{:S(2)}, u32[]{:S(2)}) %all-to-all-start.1) | async-done | bytes 1048608 | tf_op jit(solution)/shard_map/all_to_all | solution.py:67
  63.7 1.6 copy.44
  65.3 2.4 %select_reduce_fusion.1 = (f32[2,128]{1,0:T(2,128)S(1)}, f32[2,128,2048]{1,2,0:T(8,128)S(1)}) fusion(pred[128,2048]{0,1:T(8,128)(4,1)S(1)} %copy.40, f32[2,128,2048]{1,2,0:T(8,128)} %bitcast.78, bf16[2048,2,24]{0,2,1:T(8,128)(2,1)} %reshape_squeeze.6, bf16[128,2,24]{0,2,1:T(8,128)(2,1)S(1)} %bitcast.76), kind=kOutput, calls=%fused_computation.28 | convolution fusion | flops 27262720 | bytes 4666368 | tf_op jit(solution)/shard_map/qhd,khd->hqk/dot_general | solution.py:70
  68.2 1.5 fusion.31
  69.8 1.6 fusion.17
  71.3 9.5 %copy.50 = bf16[2,128,2048]{1,0,2:T(2,128)(2,1)} copy(bf16[2,128,2048]{1,2,0:T(8,128)(2,1)S(1)} %fusion.17) | data formatting | bytes 2097152 | tf_op jit(solution)/shard_map/convert_element_type | solution.py:86
  80.8 5.3 %all-to-all-start.2 = ((bf16[2,128,2048]{1,0,2:T(2,128)(2,1)}), bf16[2,128,2048]{1,0,2:T(2,128)(2,1)}, u32[]{:S(2)}, u32[]{:S(2)}) async-start(bf16[2,128,2048]{1,0,2:T(2,128)(2,1)} %copy.50), calls=%async_computation.3 | async-start | bytes 2097152 | tf_op jit(solution)/shard_map/all_to_all | solution.py:103
  87.0 1.4 fusion.38
  89.5 1.8 fusion.30
  91.3 9.4 %all-to-all-done.2 = bf16[2,128,2048]{1,0,2:T(2,128)(2,1)} async-done(((bf16[2,128,2048]{1,0,2:T(2,128)(2,1)}), bf16[2,128,2048]{1,0,2:T(2,128)(2,1)}, u32[]{:S(2)}, u32[]{:S(2)}) %all-to-all-start.2) | async-done | bytes 1048608 | tf_op jit(solution)/shard_map/all_to_all | solution.py:103
  100.7 4.2 %copy.51 = bf16[2,128,8,256]{3,0,2,1:T(2,128)(2,1)S(1)} copy(bf16[2,128,8,256]{1,0,3,2:T(2,128)(2,1)} %bitcast.22) | data formatting | bytes 2097152 | tf_op jit(solution)/shard_map/all_to_all | solution.py:103
  105.3 6.1 %fusion.25 = f32[128,16]{1,0:T(8,128)S(1)} fusion(bf16[16,128,256]{2,0,1:T(8,128)(2,1)S(1)} %all_to_all.28, bf16[128,256,128]{1,2,0:T(8,128)(2,1)} %copy.41, f32[128]{0:T(128)} %param.14, f32[128,256]{1,0:T(8,128)} %copy-done.3, f32[128,256]{1,0:T(8,128)S(1)} %broadcast_multiply_fusion.2), kind=kOutput, calls=%fused_computation.34 | convolution fusion | flops 155189248 | bytes 9708032 | tf_op jit(solution)/shard_map/ijc,hij->ch/dot_general | solution.py:108
  111.5 12.2 %fusion.11 = (f32[128]{0:T(128)S(1)}, f32[128,256]{1,0:T(8,128)S(1)}, f32[128,256]{1,0:T(8,128)S(1)}, f32[128,256,128]{1,2,0:T(8,128)}) fusion(bf16[128,256,128]{1,2,0:T(8,128)(2,1)} %copy.41, f32[128,256]{1,0:T(8,128)S(1)} %copy-done.4, f32[128,256]{1,0:T(8,128)S(1)} %broadcast_multiply_fusion.2, f32[128]{0:T(128)S(1)} %copy-done.7, ...), kind=kOutput, calls=%fused_computation.13 | convolution fusion | flops 171900800 | bytes 26743808 | tf_op jit(solution)/shard_map/hij,ch->ijc/dot_general | solution.py:104
  123.8 20.4 %psum.7 = f32[1,2176]{1,0:T(1,128)S(1)} all-reduce(f32[1,2176]{1,0:T(1,128)S(1)} %all_gather.6), channel_id=1, replica_groups=mesh['blk'=16,'col'=8] {'col'}, use_global_device_ids=true, to_apply=%region_9.10 | all-reduce | flops 2176 | bytes 17408 | tf_op jit(solution)/shard_map/psum | solution.py:111
  144.2 23.5 %all-gather = f32[16,1,2176]{2,1,0:T(1,128)S(1)} all-gather(f32[1,1,2176]{2,1,0:T(1,128)S(1)} %bitcast.84), channel_id=1, replica_groups=mesh['blk'=16,'col'=8] {'blk'}, dimensions={0}, use_global_device_ids=true | all-gather | bytes 147968 | tf_op jit(solution)/shard_map/all_gather | solution.py:111
  169.1 13.7 %fusion.10 = bf16[128,256,128]{1,2,0:T(8,128)(2,1)} fusion(bf16[128,256,128]{1,2,0:T(8,128)(2,1)} %copy.41, f32[128,256,128]{1,2,0:T(8,128)} %get-tuple-element.33, f32[128,256]{1,0:T(8,128)S(1)} %get-tuple-element.34, f32[128,256]{1,0:T(8,128)S(1)} %get-tuple-element.35, f32[128]{0:T(128)S(1)} %copy-done.7, f32[128,256]{1,0:T(8,128)S(1)} %copy-done.4, ...), kind=kLoop, calls=%fused_computation.12 | loop fusion | flops 37748736 | bytes 34079232 | tf_op jit(solution)/shard_map/convert_element_type | solution.py:122
  182.7 11.9 %copy.54 = bf16[128,256,128]{2,1,0:T(8,128)(2,1)} copy(bf16[128,256,128]{1,2,0:T(8,128)(2,1)} %fusion.10) | data formatting | bytes 16777216
  (58 shorter events, 10.4 us)
Async XLA Ops:
  7.2 58.2 %copy-start = (bf16[128,48]{0,1:T(8,128)(2,1)S(1)}, bf16[128,48]{0,1:T(8,128)(2,1)}, u32[]{:S(2)}) copy-start(bf16[128,48]{0,1:T(8,128)(2,1)} %param.9) | copy-start | bytes 36868
  8.7 33.0 %all-to-all-start = ((bf16[16,2,128,48]{2,3,1,0:T(8,128)(2,1)}), bf16[16,2,128,48]{2,3,1,0:T(8,128)(2,1)S(1)}, u32[]{:S(2)}, u32[]{:S(2)}) async-start(bf16[16,2,128,48]{2,3,1,0:T(8,128)(2,1)} %broadcast_in_dim.24), calls=%async_computation | async-start | bytes 786432 | tf_op jit(solution)/shard_map/all_to_all | solution.py:58
  27.5 6.1 %copy-start.2 = (bf16[128,256,128]{1,2,0:T(8,128)(2,1)S(1)}, bf16[128,256,128]{1,2,0:T(8,128)(2,1)}, u32[]{:S(2)}) copy-start(bf16[128,256,128]{1,2,0:T(8,128)(2,1)} %copy.41) | copy-start | bytes 25165828
  27.5 10.1 %copy-start.6 = (f32[128]{0:T(128)S(1)}, f32[128]{0:T(128)}, u32[]{:S(2)}) copy-start(f32[128]{0:T(128)} %param.14) | copy-start | bytes 1540
  27.5 10.1 %copy-start.10 = (bf16[128,16]{0,1:T(8,128)(2,1)S(1)}, bf16[128,16]{0,1:T(8,128)(2,1)}, u32[]{:S(2)}) copy-start(bf16[128,16]{0,1:T(8,128)(2,1)} %param.15) | copy-start | bytes 12292
  37.6 4.0 %copy-start.3 = (f32[128,256]{1,0:T(8,128)}, f32[128,256]{1,0:T(8,128)S(1)}, u32[]{:S(2)}) copy-start(f32[128,256]{1,0:T(8,128)S(1)} %add_rsqrt_fusion) | copy-start | bytes 393220
  37.7 11.2 %copy-start.8 = (s32[2048]{0:T(1024)S(1)}, s32[2048]{0:T(1024)}, u32[]{:S(2)}) copy-start(s32[2048]{0:T(1024)} %param.16) | copy-start | bytes 24580
  37.7 11.3 %copy-start.9 = (s32[16,16]{1,0:T(8,128)S(1)}, s32[16,16]{1,0:T(8,128)}, u32[]{:S(2)}) copy-start(s32[16,16]{1,0:T(8,128)} %param.17) | copy-start | bytes 3076
  41.7 22.0 %all-to-all-start.1 = ((bf16[16,128,256]{2,1,0:T(8,128)(2,1)}), bf16[16,128,256]{2,1,0:T(8,128)(2,1)S(1)}, u32[]{:S(2)}, u32[]{:S(2)}) async-start(bf16[16,128,256]{2,1,0:T(8,128)(2,1)} %copy.43), calls=%async_computation.1 | async-start | bytes 2097152 | tf_op jit(solution)/shard_map/all_to_all | solution.py:67
  65.3 4.4 %copy-start.5 = (bf16[2048,2,24]{0,2,1:T(8,128)(2,1)S(1)}, bf16[2048,2,24]{0,2,1:T(8,128)(2,1)}, u32[]{:S(2)}) copy-start(bf16[2048,2,24]{0,2,1:T(8,128)(2,1)} %reshape_squeeze.7) | copy-start | bytes 589828
  80.8 19.9 %all-to-all-start.2 = ((bf16[2,128,2048]{1,0,2:T(2,128)(2,1)}), bf16[2,128,2048]{1,0,2:T(2,128)(2,1)}, u32[]{:S(2)}, u32[]{:S(2)}) async-start(bf16[2,128,2048]{1,0,2:T(2,128)(2,1)} %copy.50), calls=%async_computation.3 | async-start | bytes 2097152 | tf_op jit(solution)/shard_map/all_to_all | solution.py:103
  86.1 108.5 %reduce-scatter.2.cloned.1.call-start = ((), (), s32[]{:S(2)}) async-start(), calls=%async_computation.4 | async-start | bytes 835584 | tf_op jit(solution)/shard_map/reduce_scatter | solution.py:99
  105.3 6.1 %copy-start.4 = (f32[128,256]{1,0:T(8,128)S(1)}, f32[128,256]{1,0:T(8,128)}, u32[]{:S(2)}) copy-start(f32[128,256]{1,0:T(8,128)} %copy-done.3) | copy-start | bytes 393220
  105.3 6.1 %copy-start.7 = (f32[128]{0:T(128)S(1)}, f32[128]{0:T(128)}, u32[]{:S(2)}) copy-start(f32[128]{0:T(128)} %param.14) | copy-start | bytes 1540
  105.3 6.1 %copy-start.11 = (bf16[128,16]{0,1:T(8,128)(2,1)S(1)}, bf16[128,16]{0,1:T(8,128)(2,1)}, u32[]{:S(2)}) copy-start(bf16[128,16]{0,1:T(8,128)(2,1)} %param.15) | copy-start | bytes 12292
  169.1 27.0 %copy-start.1 = (bf16[128,48]{0,1:T(8,128)(2,1)S(1)}, bf16[128,48]{0,1:T(8,128)(2,1)}, u32[]{:S(2)}) copy-start(bf16[128,48]{0,1:T(8,128)(2,1)} %param.9) | copy-start | bytes 36868
Sparse Core Ops, SparseCore 0:
  89.6 60.3 reduce-scatter.1

commit v3 on v2

--- a/solution.py
+++ b/solution.py
@@ -3,20 +3,106 @@
 import jax
 import jax.numpy as jnp
 from jax import lax
+from jax.experimental import pallas as pl
+from jax.experimental.pallas import tpu as pltpu
 from jax.sharding import PartitionSpec as P
 
 HEAD_DIM = 24
 MASK_BLOCK = 128
-
-
-def pair_norm(pair_rows, norm_gain):
-    values = pair_rows.astype(jnp.float32)
-    centre = jnp.mean(values, axis=-1, keepdims=True)
-    shifted = values - centre
+ROWS_PER_STEP = 8
+
+
+def _norm_rows(x, gain):
+    centre = jnp.mean(x, axis=-1, keepdims=True)
+    shifted = x - centre
     inverse = lax.rsqrt(jnp.mean(shifted * shifted, axis=-1, keepdims=True) + 1e-05)
     unit = shifted * inverse
-    normed = (unit * norm_gain).astype(jnp.bfloat16)
-    return (unit, inverse, normed)
+    return unit, inverse, (unit * gain).astype(jnp.bfloat16)
+
+
+def _bias_kernel(pair_ref, gain_ref, wt_ref, bias_ref):
+    gain = gain_ref[...]
+    wt = wt_ref[...]
+    for r in range(pair_ref.shape[0]):
+        _, _, normed = _norm_rows(pair_ref[r].astype(jnp.float32), gain)
+        bias = lax.dot_general(
+            wt, normed, (((1,), (1,)), ((), ())), preferred_element_type=jnp.float32
+        )
+        bias_ref[r] = bias.astype(jnp.bfloat16)
+
+
+def pair_bias(pair_rep, norm_gain, bias_weight):
+    rows, cols, width = pair_rep.shape
+    heads = bias_weight.shape[1]
+    step = ROWS_PER_STEP
+    return pl.pallas_call(
+        _bias_kernel,
+        out_shape=jax.ShapeDtypeStruct((rows, heads, cols), jnp.bfloat16),
+        grid=(rows // step,),
+        in_specs=[
+            pl.BlockSpec((step, cols, width), lambda i: (i, 0, 0)),
+            pl.BlockSpec((1, width), lambda i: (0, 0)),
+            pl.BlockSpec((heads, width), lambda i: (0, 0)),
+        ],
+        out_specs=pl.BlockSpec((step, heads, cols), lambda i: (i, 0, 0)),
+        compiler_params=pltpu.CompilerParams(dimension_semantics=("arbitrary",)),
+    )(pair_rep, norm_gain.reshape(1, width).astype(jnp.float32), bias_weight.T)
+
+
+def _grad_kernel(pair_ref, ds_ref, gain_ref, wt_ref, gp_ref, gw_ref, gg_ref):
+    @pl.when(pl.program_id(0) == 0)
+    def _():
+        gw_ref[...] = jnp.zeros_like(gw_ref)
+        gg_ref[...] = jnp.zeros_like(gg_ref)
+
+    gain = gain_ref[...]
+    wt = wt_ref[...]
+    gw = jnp.zeros(gw_ref.shape, jnp.float32)
+    gg = jnp.zeros(gg_ref.shape, jnp.float32)
+    for r in range(pair_ref.shape[0]):
+        unit, inverse, normed = _norm_rows(pair_ref[r].astype(jnp.float32), gain)
+        ds = ds_ref[r]
+        dnormed = lax.dot_general(
+            ds, wt, (((0,), (0,)), ((), ())), preferred_element_type=jnp.float32
+        )
+        gw = gw + jnp.dot(ds, normed, preferred_element_type=jnp.float32)
+        gg = gg + jnp.sum(dnormed * unit, axis=0, keepdims=True)
+        scaled = dnormed * gain
+        grad = inverse * (
+            scaled
+            - jnp.mean(scaled, axis=-1, keepdims=True)
+            - unit * jnp.mean(scaled * unit, axis=-1, keepdims=True)
+        )
+        gp_ref[r] = grad.astype(jnp.bfloat16)
+    gw_ref[...] += gw
+    gg_ref[...] += gg
+
+
+def pair_grads(pair_rep, dbias, norm_gain, bias_weight):
+    rows, cols, width = pair_rep.shape
+    heads = bias_weight.shape[1]
+    step = ROWS_PER_STEP
+    return pl.pallas_call(
+        _grad_kernel,
+        out_shape=(
+            jax.ShapeDtypeStruct((rows, cols, width), jnp.bfloat16),
+            jax.ShapeDtypeStruct((heads, width), jnp.float32),
+            jax.ShapeDtypeStruct((1, width), jnp.float32),
+        ),
+        grid=(rows // step,),
+        in_specs=[
+            pl.BlockSpec((step, cols, width), lambda i: (i, 0, 0)),
+            pl.BlockSpec((step, heads, cols), lambda i: (i, 0, 0)),
+            pl.BlockSpec((1, width), lambda i: (0, 0)),
+            pl.BlockSpec((heads, width), lambda i: (0, 0)),
+        ],
+        out_specs=(
+            pl.BlockSpec((step, cols, width), lambda i: (i, 0, 0)),
+            pl.BlockSpec((heads, width), lambda i: (0, 0)),
+            pl.BlockSpec((1, width), lambda i: (0, 0)),
+        ),
+        compiler_params=pltpu.CompilerParams(dimension_semantics=("arbitrary",)),
+    )(pair_rep, dbias, norm_gain.reshape(1, width).astype(jnp.float32), bias_weight.T)
 
 
 def block_onehot(first_token, count, nblocks):
@@ -52,7 +138,6 @@
     )
     allowed = (hits > 0.5) | (chain_rows[:, None] == chain_ids[None, :])
 
-    unit, inverse, normed = pair_norm(pair_rep, norm_gain)
     kv_local = jnp.stack([key_proj, value_proj])
     kv_rep = jnp.broadcast_to(kv_local[None], (blk_count,) + kv_local.shape)
     kv_all = lax.all_to_all(kv_rep, "blk", split_axis=0, concat_axis=0, tiled=True)
@@ -61,10 +146,9 @@
     grad_heads = out_grad.reshape(tok_rows, local_heads, HEAD_DIM)
     key_heads = kv_all[0].reshape(all_tokens, local_heads, HEAD_DIM)
     value_heads = kv_all[1].reshape(all_tokens, local_heads, HEAD_DIM)
-    bias_local = jnp.einsum(
-        "ijc,ch->hij", normed, bias_weight, preferred_element_type=jnp.float32
-    ).astype(jnp.bfloat16)
-    bias_mine = lax.all_to_all(bias_local, "col", split_axis=0, concat_axis=2, tiled=True)
+    bias_local = pair_bias(pair_rep, norm_gain, bias_weight)
+    bias_mine = lax.all_to_all(bias_local, "col", split_axis=1, concat_axis=2, tiled=True)
+    bias_mine = jnp.transpose(bias_mine, (1, 0, 2))
 
     scores = (
         jnp.einsum("qhd,khd->hqk", query_heads, key_heads, preferred_element_type=jnp.float32)
@@ -100,26 +184,15 @@
     grad_queries = query_add.reshape(tok_rows, local_width).astype(jnp.bfloat16)
     grad_keys = kv_grads[0].astype(jnp.bfloat16)
     grad_values = kv_grads[1].astype(jnp.bfloat16)
-    dbias_cells = lax.all_to_all(dscores, "col", split_axis=2, concat_axis=0, tiled=True)
-    dnormed = jnp.einsum(
-        "hij,ch->ijc", dbias_cells, bias_weight, preferred_element_type=jnp.float32
-    )
-    gain_part = jnp.sum(dnormed * unit, axis=(0, 1))
-    weight_part = jnp.einsum("ijc,hij->ch", normed, dbias_cells, preferred_element_type=jnp.float32)
-    pair_width = gain_part.shape[0]
-    packed = jnp.concatenate([gain_part, weight_part.reshape(-1)])
+    dbias_cells = lax.all_to_all(
+        jnp.transpose(dscores, (1, 0, 2)), "col", split_axis=2, concat_axis=1, tiled=True
+    )
+    grad_pair, weight_part, gain_part = pair_grads(pair_rep, dbias_cells, norm_gain, bias_weight)
+    pair_width = gain_part.shape[1]
+    packed = jnp.concatenate([gain_part[0], weight_part.T.reshape(-1)])
     packed = jnp.sum(lax.all_gather(lax.psum(packed, "col"), "blk"), axis=0)
     grad_gain = packed[:pair_width]
-    grad_weight = packed[pair_width:].reshape(weight_part.shape)
-    scaled = dnormed * norm_gain
-    grad_pair = (
-        inverse
-        * (
-            scaled
-            - jnp.mean(scaled, axis=-1, keepdims=True)
-            - unit * jnp.mean(scaled * unit, axis=-1, keepdims=True)
-        )
-    ).astype(jnp.bfloat16)
+    grad_weight = packed[pair_width:].reshape(weight_part.shape[::-1])
     return (grad_queries, grad_keys, grad_values, grad_pair, grad_gain, grad_weight)
 
 

time: 204 us -> 196 us (0.961)
  Pallas kernels: 0 us -> 55.1 us
  local copies, waits for them, and re-layouts: 45.9 us -> 21.9 us
  matrix products: 31.2 us -> 8.7 us
  other arithmetic: 26.8 us -> 6.62 us
  waiting for transfers between devices: 21.1 us -> 26 us
    pallas_call x0 -> x2, Pallas kernels: none -> 55.1 us  [the longest x1 37.6 us: pair_grads(): pl.pallas_call(_grad_kernel, out_shape=(jax.ShapeDtypeStruct((rows, cols,...]
    unnamed x27 -> x13, local copies, waits for them, and re-layouts: 24.6 us -> 0.96 us
    dot_general x3 -> x0, matrix products: 21 us -> none  [the longest x1 12.2 us: local(): jnp.einsum('hij,ch->ijc', dbias_cells, bias_weight, preferred_element_typ...]
    convert_element_type x1, other arithmetic: 13.7 us -> 2.89 us  [local(): (probs.astype(jnp.float32) * (dprobs - delta[:, :, None])).astype(jnp.bfl...]
    reduce_sum x2 -> x0, other arithmetic: 10 us -> none  [the longest x1 6.06 us: pair_norm(): centre = jnp.mean(values, axis=-1, keepdims=True)]
    all_to_all x2, waiting for transfers between devices: 21.1 us -> 26 us  [the longest x1 14.3 us: local(): lax.all_to_all(jnp.transpose(dscores, (1, 0, 2)), 'col', split_axis=2, co...]
    pallas_call x0 -> x1, local copies, waits for them, and re-layouts: none -> 2.56 us  [pair_bias(): pl.pallas_call(_bias_kernel, out_shape=jax.ShapeDtypeStruct((rows, heads,...]
  transfers between devices with their start and end apart: 4 -> 4, of which waited for: 2 -> 2; matrix products, arithmetic and copies ran while one was open for 41% -> 12% of each run, Pallas kernels for 0% -> 28%
where the time goes in v3:
time: 196 us; the launch traced here: 195 us
  Pallas kernels  55.1 us (28%)
  blocking collectives  43.1 us (22%)
  waiting for transfers between devices  26 us (13%)
  local copies, waits for them, and re-layouts  21.9 us (11%)
  starting transfers between devices  19.5 us (10%)
  between operations  14.2 us (7%)
  matrix products  8.7 us (4%)
  other arithmetic  6.62 us (3%)
    pallas_call x1, Pallas kernels, pair_grads(): pl.pallas_call(_grad_kernel, out_shape=(jax.ShapeDtypeStruct((rows, cols,...  37.6 us
    all_gather x1, blocking collectives, local(): packed = jnp.sum(lax.all_gather(lax.psum(packed, 'col'), 'blk'), axis=0)  23.5 us
    psum x1, blocking collectives, local(): packed = jnp.sum(lax.all_gather(lax.psum(packed, 'col'), 'blk'), axis=0)  19.6 us
    pallas_call x1, Pallas kernels, pair_bias(): pl.pallas_call(_bias_kernel, out_shape=jax.ShapeDtypeStruct((rows, heads,...  17.5 us
    all_to_all x1, waiting for transfers between devices, local(): lax.all_to_all(jnp.transpose(dscores, (1, 0, 2)), 'col', split_axis=2, co...  14.3 us
    all_to_all x1, waiting for transfers between devices, local(): lax.all_to_all(bias_local, 'col', split_axis=1, concat_axis=2, tiled=True)  11.7 us
    convert_element_type x1, local copies, waits for them, and re-layouts, local(): (probs.astype(jnp.float32) * (dprobs - delta[:, :, None])).astype(jnp.bfl...  9.46 us
    all_to_all x1, starting transfers between devices, local(): lax.all_to_all(bias_local, 'col', split_axis=1, concat_axis=2, tiled=True)  7.2 us
  transfers between devices with their start and end apart: 4, of which 2 were waited for; matrix products, arithmetic and copies ran while one was open for 12% of the time, Pallas kernels for 28%

profile of v3, /device:TPU:1, one launch (start us, length us, event | category | flops | bytes accessed | tf_op | source)
XLA Modules:
  0.0 195.1 jit_solution(10841491038873130567)
XLA Ops:
  7.9 0.8 broadcast_in_dim.44
  8.7 6.9 %all-to-all-start = ((bf16[16,2,128,48]{2,3,1,0:T(8,128)(2,1)}), bf16[16,2,128,48]{2,3,1,0:T(8,128)(2,1)S(1)}, u32[]{:S(2)}, u32[]{:S(2)}) async-start(bf16[16,2,128,48]{2,3,1,0:T(8,128)(2,1)} %broadcast_in_dim.44), calls=%async_computation | async-start | bytes 786432 | tf_op jit(solution)/shard_map/all_to_all | solution.py:143
  15.6 17.5 %shard_map.136 = bf16[128,16,256]{2,1,0:T(8,128)(2,1)} custom-call(bf16[128,256,128]{2,1,0:T(8,128)(2,1)} %pair_ref.3, f32[1,128]{1,0:T(1,128)} %bitcast.108, bf16[16,128]{1,0:T(8,128)(2,1)} %bitcast.101), custom_call_target="tpu_custom_call" | custom-call | tf_op jit(solution)/shard_map/pallas_call | solution.py:38
  33.1 2.6 %copy.35 = bf16[128,16,256]{2,0,1:T(8,128)(2,1)} copy(bf16[128,16,256]{2,1,0:T(8,128)(2,1)} %shard_map.136) | data formatting | bytes 2097152 | tf_op jit(solution)/shard_map/pallas_call | solution.py:38
  35.7 7.2 %all-to-all-start.1 = ((bf16[128,16,256]{2,0,1:T(8,128)(2,1)}), bf16[128,16,256]{2,0,1:T(8,128)(2,1)S(1)}, u32[]{:S(2)}, u32[]{:S(2)}) async-start(bf16[128,16,256]{2,0,1:T(8,128)(2,1)} %copy.35), calls=%async_computation.1 | async-start | bytes 2097152 | tf_op jit(solution)/shard_map/all_to_all | solution.py:150
  43.1 0.8 fusion
  44.4 0.8 reshape_squeeze.6
  45.3 0.8 reshape_squeeze.7
  46.0 11.7 %all-to-all-done.1 = bf16[128,16,256]{2,0,1:T(8,128)(2,1)S(1)} async-done(((bf16[128,16,256]{2,0,1:T(8,128)(2,1)}), bf16[128,16,256]{2,0,1:T(8,128)(2,1)S(1)}, u32[]{:S(2)}, u32[]{:S(2)}) %all-to-all-start.1) | async-done | bytes 1048608 | tf_op jit(solution)/shard_map/all_to_all | solution.py:150
  58.2 3.0 %select_reduce_fusion.1 = (f32[2,128]{1,0:T(2,128)S(1)}, f32[2,128,2048]{1,2,0:T(8,128)S(1)}, f32[2,2048,128]{2,1,0:T(8,128)}) fusion(pred[128,2048]{0,1:T(8,128)(4,1)S(1)} %copy.34, f32[128,8,2,256]{0,3,1,2:T(8,128)S(1)} %copy.36, bf16[2048,2,24]{0,2,1:T(8,128)(2,1)} %reshape_squeeze.6, bf16[128,2,24]{0,2,1:T(8,128)(2,1)S(1)} %bitcast.88), kind=kOutput, calls=%fused_computation.17 | convolution fusion | flops 27262720 | bytes 6763520 | tf_op jit(solution)/shard_map/qhd,khd->hqk/dot_general | solution.py:154
  63.2 2.1 %fusion.7 = (bf16[2,128,2048]{1,2,0:T(8,128)(2,1)S(1)}, f32[2,2048,128]{2,1,0:T(8,128)}) fusion(f32[2,128]{1,0:T(2,128)S(1)} %bitcast.107, f32[2,128,2048]{1,2,0:T(8,128)S(1)} %get-tuple-element.25, f32[2,128]{1,0:T(2,128)S(1)} %log_add_fusion, pred[128,2048]{0,1:T(8,128)(4,1)S(1)} %copy.34, bf16[2048,2,24]{0,2,1:T(8,128)(2,1)S(1)} %copy-done.2, ...), kind=kOutput, calls=%fused_computation.14 | convolution fusion | flops 28835840 | bytes 5715968 | tf_op jit(solution)/shard_map/qhd,khd->hqk/dot_general | solution.py:167
  65.9 1.0 pad_maximum_fusion
  67.0 2.9 %fusion.2 = bf16[128,2,2048]{0,2,1:T(8,128)(2,1)S(1)} fusion(f32[2,2048,128]{2,1,0:T(8,128)} %get-tuple-element.32, f32[128,8,2,256]{0,3,1,2:T(8,128)S(1)} %copy.36, f32[2,2048,128]{2,1,0:T(8,128)} %get-tuple-element.30, f32[128,2]{0,1:T(2,128)S(1)} %fusion.13, f32[128,2]{0,1:T(2,128)S(1)} %bitcast.100, pred[128,2048]{0,1:T(8,128)(4,1)S(1)} %copy.34), kind=kLoop, calls=%fused_computation.7 | loop fusion | flops 4194304 | bytes 7604224 | tf_op jit(solution)/shard_map/convert_element_type | solution.py:170
  69.9 9.5 %copy.43 = bf16[128,2,2048]{0,1,2:T(2,128)(2,1)} copy(bf16[128,2,2048]{0,2,1:T(8,128)(2,1)S(1)} %fusion.2) | data formatting | bytes 2097152 | tf_op jit(solution)/shard_map/convert_element_type | solution.py:170
  79.3 5.3 %all-to-all-start.2 = ((bf16[128,2,2048]{0,1,2:T(2,128)(2,1)}), bf16[128,2,2048]{0,1,2:T(2,128)(2,1)S(1)}, u32[]{:S(2)}, u32[]{:S(2)}) async-start(bf16[128,2,2048]{0,1,2:T(2,128)(2,1)} %copy.43), calls=%async_computation.3 | async-start | bytes 2097152 | tf_op jit(solution)/shard_map/all_to_all | solution.py:187
  84.7 0.9 fusion.12
  85.5 14.3 %all-to-all-done.2 = bf16[128,2,2048]{0,1,2:T(2,128)(2,1)S(1)} async-done(((bf16[128,2,2048]{0,1,2:T(2,128)(2,1)}), bf16[128,2,2048]{0,1,2:T(2,128)(2,1)S(1)}, u32[]{:S(2)}, u32[]{:S(2)}) %all-to-all-start.2) | async-done | bytes 1048608 | tf_op jit(solution)/shard_map/all_to_all | solution.py:187
  99.9 2.1 %copy.44 = bf16[128,2,8,256]{3,1,2,0:T(2,128)(2,1)S(1)} copy(bf16[128,2,8,256]{0,1,3,2:T(2,128)(2,1)S(1)} %bitcast.91) | data formatting | bytes 2097152 | tf_op jit(solution)/shard_map/all_to_all | solution.py:187
  102.0 1.2 all_to_all.28.ds_ref
  103.2 37.6 %shard_map.137 = (bf16[128,256,128]{2,1,0:T(8,128)(2,1)}, f32[16,128]{1,0:T(8,128)}, f32[1,128]{1,0:T(1,128)}) custom-call(bf16[128,256,128]{2,1,0:T(8,128)(2,1)} %pair_ref.3, bf16[128,16,256]{2,1,0:T(8,128)(2,1)} %all_to_all.28.ds_ref, f32[1,128]{1,0:T(1,128)} %bitcast.109, bf16[16,128]{1,0:T(8,128)(2,1)} %bitcast.102), custom_call_target="tpu_custom_call" | custom-call | tf_op jit(solution)/shard_map/pallas_call | solution.py:85
  140.8 0.8 copy.45
  142.3 19.6 %psum.7 = f32[1,2176]{1,0:T(1,128)S(1)} all-reduce(f32[1,2176]{1,0:T(1,128)S(1)} %all_gather.6), channel_id=1, replica_groups=mesh['blk'=16,'col'=8] {'col'}, use_global_device_ids=true, to_apply=%region_4.5 | all-reduce | flops 2176 | bytes 17408 | tf_op jit(solution)/shard_map/psum | solution.py:193
  161.9 23.5 %all-gather = f32[16,1,2176]{2,1,0:T(1,128)S(1)} all-gather(f32[1,1,2176]{2,1,0:T(1,128)S(1)} %bitcast.99), channel_id=1, replica_groups=mesh['blk'=16,'col'=8] {'blk'}, dimensions={0}, use_global_device_ids=true | all-gather | bytes 147968 | tf_op jit(solution)/shard_map/all_gather | solution.py:193
  186.8 0.8 convert.11
  (39 shorter events, 7.4 us)
Async XLA Ops:
  7.2 51.1 %copy-start = (bf16[128,48]{0,1:T(8,128)(2,1)S(1)}, bf16[128,48]{0,1:T(8,128)(2,1)}, u32[]{:S(2)}) copy-start(bf16[128,48]{0,1:T(8,128)(2,1)} %param.9) | copy-start | bytes 36868
  8.7 27.0 %all-to-all-start = ((bf16[16,2,128,48]{2,3,1,0:T(8,128)(2,1)}), bf16[16,2,128,48]{2,3,1,0:T(8,128)(2,1)S(1)}, u32[]{:S(2)}, u32[]{:S(2)}) async-start(bf16[16,2,128,48]{2,3,1,0:T(8,128)(2,1)} %broadcast_in_dim.44), calls=%async_computation | async-start | bytes 786432 | tf_op jit(solution)/shard_map/all_to_all | solution.py:143
  33.1 9.8 %copy-start.4 = (s32[2048]{0:T(1024)S(1)}, s32[2048]{0:T(1024)}, u32[]{:S(2)}) copy-start(s32[2048]{0:T(1024)} %param.16) | copy-start | bytes 24580
  33.1 9.9 %copy-start.5 = (s32[16,16]{1,0:T(8,128)S(1)}, s32[16,16]{1,0:T(8,128)}, u32[]{:S(2)}) copy-start(s32[16,16]{1,0:T(8,128)} %param.17) | copy-start | bytes 3076
  35.7 22.0 %all-to-all-start.1 = ((bf16[128,16,256]{2,0,1:T(8,128)(2,1)}), bf16[128,16,256]{2,0,1:T(8,128)(2,1)S(1)}, u32[]{:S(2)}, u32[]{:S(2)}) async-start(bf16[128,16,256]{2,0,1:T(8,128)(2,1)} %copy.35), calls=%async_computation.1 | async-start | bytes 2097152 | tf_op jit(solution)/shard_map/all_to_all | solution.py:150
  42.9 143.9 %reduce-scatter.2.cloned.1.call-start = ((), (), s32[]{:S(2)}) async-start(), calls=%async_computation.4 | async-start | bytes 835584 | tf_op jit(solution)/shard_map/reduce_scatter | solution.py:183
  61.2 0.7 copy-start.3
  61.2 1.4 copy-start.2
  69.9 14.8 %copy-start.1 = (bf16[2048,2,24]{0,2,1:T(8,128)(2,1)S(1)}, bf16[2048,2,24]{0,2,1:T(8,128)(2,1)}, u32[]{:S(2)}) copy-start(bf16[2048,2,24]{0,2,1:T(8,128)(2,1)} %reshape_squeeze.6) | copy-start | bytes 589828
  79.3 20.6 %all-to-all-start.2 = ((bf16[128,2,2048]{0,1,2:T(2,128)(2,1)}), bf16[128,2,2048]{0,1,2:T(2,128)(2,1)S(1)}, u32[]{:S(2)}, u32[]{:S(2)}) async-start(bf16[128,2,2048]{0,1,2:T(2,128)(2,1)} %copy.43), calls=%async_computation.3 | async-start | bytes 2097152 | tf_op jit(solution)/shard_map/all_to_all | solution.py:187
Sparse Core Ops, SparseCore 0:
  67.1 59.1 reduce-scatter.1

commit v4 on v3

v4 whole, which is shorter than its diff:
```python
import math

import jax
import jax.numpy as jnp
from jax import lax
from jax.experimental import pallas as pl
from jax.experimental.pallas import tpu as pltpu
from jax.sharding import PartitionSpec as P

HEAD_DIM = 24
MASK_BLOCK = 128
ROWS_PER_STEP = 8
CHUNKS = 1


def _norm_rows(x, gain):
    centre = jnp.mean(x, axis=-1, keepdims=True)
    shifted = x - centre
    inverse = lax.rsqrt(jnp.mean(shifted * shifted, axis=-1, keepdims=True) + 1e-05)
    unit = shifted * inverse
    return unit, inverse, (unit * gain).astype(jnp.bfloat16)


def _bias_kernel(pair_ref, gain_ref, wt_ref, bias_ref):
    gain = gain_ref[...]
    wt = wt_ref[...]
    for r in range(pair_ref.shape[0]):
        _, _, normed = _norm_rows(pair_ref[r].astype(jnp.float32), gain)
        bias = lax.dot_general(
            wt, normed, (((1,), (1,)), ((), ())), preferred_element_type=jnp.float32
        )
        bias_ref[r] = bias.astype(jnp.bfloat16)


def pair_bias(pair_rep, norm_gain, bias_weight, first, count):
    _, cols, width = pair_rep.shape
    heads = bias_weight.shape[1]
    step = ROWS_PER_STEP
    base = first // step
    return pl.pallas_call(
        _bias_kernel,
        out_shape=jax.ShapeDtypeStruct((count, heads, cols), jnp.bfloat16),
        grid=(count // step,),
        in_specs=[
            pl.BlockSpec((step, cols, width), lambda i: (i + base, 0, 0)),
            pl.BlockSpec((1, width), lambda i: (0, 0)),
            pl.BlockSpec((heads, width), lambda i: (0, 0)),
        ],
        out_specs=pl.BlockSpec((step, heads, cols), lambda i: (i, 0, 0)),
        compiler_params=pltpu.CompilerParams(dimension_semantics=("arbitrary",)),
    )(pair_rep, norm_gain.reshape(1, width).astype(jnp.float32), bias_weight.T)


def _grad_kernel(pair_ref, ds_ref, gain_ref, wt_ref, *refs):
    gp_ref, gw_ref, gg_ref = refs[-3:]

    @pl.when(pl.program_id(0) == 0)
    def _():
        gw_ref[...] = jnp.zeros_like(gw_ref)
        gg_ref[...] = jnp.zeros_like(gg_ref)

    gain = gain_ref[...]
    wt = wt_ref[...]
    gw = jnp.zeros(gw_ref.shape, jnp.float32)
    gg = jnp.zeros(gg_ref.shape, jnp.float32)
    for r in range(pair_ref.shape[0]):
        unit, inverse, normed = _norm_rows(pair_ref[r].astype(jnp.float32), gain)
        ds = ds_ref[r]
        ds_t = ds.astype(jnp.float32).T.astype(jnp.bfloat16)
        dnormed = jnp.dot(ds_t, wt, preferred_element_type=jnp.float32)
        gw = gw + jnp.dot(ds, normed, preferred_element_type=jnp.float32)
        gg = gg + jnp.sum(dnormed * unit, axis=0, keepdims=True)
        scaled = dnormed * gain
        grad = inverse * (
            scaled
            - jnp.mean(scaled, axis=-1, keepdims=True)
            - unit * jnp.mean(scaled * unit, axis=-1, keepdims=True)
        )
        gp_ref[r] = grad.astype(jnp.bfloat16)
    gw_ref[...] += gw
    gg_ref[...] += gg


def pair_grads(pair_rep, dbias, norm_gain, bias_weight, first, into):
    rows, cols, width = pair_rep.shape
    count = dbias.shape[0]
    heads = bias_weight.shape[1]
    step = ROWS_PER_STEP
    base = first // step
    operands = [pair_rep, dbias, norm_gain.reshape(1, width).astype(jnp.float32), bias_weight.T]
    in_specs = [
        pl.BlockSpec((step, cols, width), lambda i: (i + base, 0, 0)),
        pl.BlockSpec((step, heads, cols), lambda i: (i, 0, 0)),
        pl.BlockSpec((1, width), lambda i: (0, 0)),
        pl.BlockSpec((heads, width), lambda i: (0, 0)),
    ]
    aliases = {}
    if into is not None:
        aliases = {len(operands): 0}
        operands.append(into)
        in_specs.append(pl.BlockSpec(memory_space=pl.ANY))
    return pl.pallas_call(
        _grad_kernel,
        out_shape=(
            jax.ShapeDtypeStruct((rows, cols, width), jnp.bfloat16),
            jax.ShapeDtypeStruct((heads, width), jnp.float32),
            jax.ShapeDtypeStruct((1, width), jnp.float32),
        ),
        grid=(count // step,),
        in_specs=in_specs,
        out_specs=(
            pl.BlockSpec((step, cols, width), lambda i: (i + base, 0, 0)),
            pl.BlockSpec((heads, width), lambda i: (0, 0)),
            pl.BlockSpec((1, width), lambda i: (0, 0)),
        ),
        input_output_aliases=aliases,
        compiler_params=pltpu.CompilerParams(dimension_semantics=("arbitrary",)),
    )(*operands)


def block_onehot(first_token, count, nblocks):
    block_ids = (first_token + jnp.arange(count, dtype=jnp.int32)) // MASK_BLOCK
    return (block_ids[:, None] == jnp.arange(nblocks, dtype=jnp.int32)[None, :]).astype(
        jnp.bfloat16
    )


def local(
    queries, key_proj, value_proj, out_grad, pair_rep, norm_gain, bias_weight, chain_ids, block_mask
):
    tok_rows = queries.shape[0]
    local_width = queries.shape[1]
    local_heads = local_width // HEAD_DIM
    scale_factor = 1.0 / math.sqrt(HEAD_DIM)
    blk_index = lax.axis_index("blk")
    blk_count = lax.axis_size("blk")
    all_tokens = blk_count * tok_rows
    row_start = blk_index * tok_rows
    nblocks = block_mask.shape[0]
    count = tok_rows // CHUNKS
    firsts = [c * count for c in range(CHUNKS)]

    kv_local = jnp.stack([key_proj, value_proj])
    kv_rep = jnp.broadcast_to(kv_local[None], (blk_count,) + kv_local.shape)
    kv_all = lax.all_to_all(kv_rep, "blk", split_axis=0, concat_axis=0, tiled=True)
    kv_all = jnp.transpose(kv_all, (1, 0, 2, 3)).reshape(2, all_tokens, local_width)
    key_heads = kv_all[0].reshape(all_tokens, local_heads, HEAD_DIM)
    value_heads = kv_all[1].reshape(all_tokens, local_heads, HEAD_DIM)

    bias_parts = []
    for first in firsts:
        bias_local = pair_bias(pair_rep, norm_gain, bias_weight, first, count)
        bias_mine = lax.all_to_all(bias_local, "col", split_axis=1, concat_axis=2, tiled=True)
        bias_parts.append(jnp.transpose(bias_mine, (1, 0, 2)))

    column_table = block_onehot(0, all_tokens, nblocks)
    query_grads, kv_parts, dbias_parts = [], [], []
    for first, bias_mine in zip(firsts, bias_parts):
        rows_table = jnp.dot(
            block_onehot(row_start + first, count, nblocks),
            block_mask.astype(jnp.bfloat16),
            preferred_element_type=jnp.float32,
        ).astype(jnp.bfloat16)
        chain_rows = lax.dynamic_slice_in_dim(chain_ids, row_start + first, count)
        hits = lax.dot_general(
            rows_table, column_table, (((1,), (1,)), ((), ())), preferred_element_type=jnp.float32
        )
        allowed = (hits > 0.5) | (chain_rows[:, None] == chain_ids[None, :])
        query_heads = queries[first : first + count].reshape(count, local_heads, HEAD_DIM)
        grad_heads = out_grad[first : first + count].reshape(count, local_heads, HEAD_DIM)

        scores = (
            jnp.einsum("qhd,khd->hqk", query_heads, key_heads, preferred_element_type=jnp.float32)
            * scale_factor
            + bias_mine.astype(jnp.float32)
        )
        masked = jnp.where(allowed[None], scores, -jnp.inf)
        row_top = jnp.max(masked, axis=-1, keepdims=True)
        expo = jnp.where(allowed[None], jnp.exp(scores - row_top), 0.0)
        totals = jnp.sum(expo, axis=-1, keepdims=True)
        log_total = row_top + jnp.log(totals)
        weights = jnp.where(allowed[None], jnp.exp(scores - log_total), 0.0)
        probs = weights.astype(jnp.bfloat16)
        attended = jnp.einsum("hqk,khd->qhd", weights, value_heads.astype(jnp.float32))
        delta = jnp.sum(grad_heads.astype(jnp.float32) * attended, axis=-1).T
        dprobs = jnp.einsum(
            "qhd,khd->hqk", grad_heads, value_heads, preferred_element_type=jnp.float32
        )
        dscores = (probs.astype(jnp.float32) * (dprobs - delta[:, :, None])).astype(jnp.bfloat16)
        dbias_parts.append(
            lax.all_to_all(
                jnp.transpose(dscores, (1, 0, 2)), "col", split_axis=2, concat_axis=1, tiled=True
            )
        )
        query_grads.append(
            jnp.einsum("hqk,khd->qhd", dscores, key_heads, preferred_element_type=jnp.float32)
            * scale_factor
        )
        key_add = (
            jnp.einsum("hqk,qhd->khd", dscores, query_heads, preferred_element_type=jnp.float32)
            * scale_factor
        )
        value_add = jnp.einsum(
            "hqk,qhd->khd", probs, grad_heads, preferred_element_type=jnp.float32
        )
        kv_parts.append(
            jnp.stack(
                [key_add.reshape(all_tokens, local_width), value_add.reshape(all_tokens, local_width)]
            )
        )
    kv_part = kv_parts[0]
    for extra in kv_parts[1:]:
        kv_part = kv_part + extra
    kv_grads = lax.psum_scatter(kv_part, "blk", scatter_dimension=1, tiled=True)
    grad_queries = jnp.concatenate(query_grads, axis=0).reshape(tok_rows, local_width)
    grad_queries = grad_queries.astype(jnp.bfloat16)
    grad_keys = kv_grads[0].astype(jnp.bfloat16)
    grad_values = kv_grads[1].astype(jnp.bfloat16)

    grad_pair = None
    weight_part = 0.0
    gain_part = 0.0
    for first, dbias_cells in zip(firsts, dbias_parts):
        grad_pair, weight_add, gain_add = pair_grads(
            pair_rep, dbias_cells, norm_gain, bias_weight, first, grad_pair
        )
        weight_part = weight_part + weight_add
        gain_part = gain_part + gain_add
    pair_width = gain_part.shape[1]
    packed = jnp.concatenate([gain_part[0], weight_part.T.reshape(-1)])
    packed = jnp.sum(lax.all_gather(lax.psum(packed, "col"), "blk"), axis=0)
    grad_gain = packed[:pair_width]
    grad_weight = packed[pair_width:].reshape(weight_part.shape[::-1])
    return (grad_queries, grad_keys, grad_values, grad_pair, grad_gain, grad_weight)


def solution(mesh):
    placed = (
        P("blk", "col"),
        P("blk", "col"),
        P("blk", "col"),
        P("blk", "col"),
        P("blk", "col", None),
        P(),
        P(),
        P(),
        P(),
    )
    return jax.shard_map(
        local,
        mesh=mesh,
        in_specs=placed,
        out_specs=(
            P("blk", "col"),
            P("blk", "col"),
            P("blk", "col"),
            P("blk", "col", None),
            P(),
            P(),
        ),
        check_vma=False,
    )
```

time: 196 us -> 194 us (0.990)
  Pallas kernels: 55.1 us -> 52.6 us
    pallas_call x1, Pallas kernels: 37.6 us -> 35.1 us  [pair_grads(): pl.pallas_call(_grad_kernel, out_shape=(jax.ShapeDtypeStruct((rows, cols,...]
  transfers between devices with their start and end apart: 4 -> 4, of which waited for: 2 -> 2; matrix products, arithmetic and copies ran while one was open for 12% -> 12% of each run, Pallas kernels for 28% -> 27%
where the time goes in v4:
time: 194 us; the launch traced here: 193 us
  Pallas kernels  52.6 us (27%)
  blocking collectives  43.1 us (22%)
  waiting for transfers between devices  26 us (13%)
  local copies, waits for them, and re-layouts  21.9 us (11%)
  starting transfers between devices  19.5 us (10%)
  between operations  14.2 us (7%)
  matrix products  8.7 us (4%)
  other arithmetic  6.62 us (3%)
    pallas_call x1, Pallas kernels, pair_grads(): pl.pallas_call(_grad_kernel, out_shape=(jax.ShapeDtypeStruct((rows, cols,...  35.1 us
    all_gather x1, blocking collectives, local(): packed = jnp.sum(lax.all_gather(lax.psum(packed, 'col'), 'blk'), axis=0)  23.5 us
    psum x1, blocking collectives, local(): packed = jnp.sum(lax.all_gather(lax.psum(packed, 'col'), 'blk'), axis=0)  19.6 us
    pallas_call x1, Pallas kernels, pair_bias(): pl.pallas_call(_bias_kernel, out_shape=jax.ShapeDtypeStruct((count, heads...  17.5 us
    all_to_all x1, waiting for transfers between devices, local(): lax.all_to_all(jnp.transpose(dscores, (1, 0, 2)), 'col', split_axis=2, co...  14.3 us
    all_to_all x1, waiting for transfers between devices, local(): lax.all_to_all(bias_local, 'col', split_axis=1, concat_axis=2, tiled=True)  11.7 us
    convert_element_type x1, local copies, waits for them, and re-layouts, local(): (probs.astype(jnp.float32) * (dprobs - delta[:, :, None])).astype(jnp.bfl...  9.46 us
    all_to_all x1, starting transfers between devices, local(): lax.all_to_all(bias_local, 'col', split_axis=1, concat_axis=2, tiled=True)  7.2 us
  transfers between devices with their start and end apart: 4, of which 2 were waited for; matrix products, arithmetic and copies ran while one was open for 12% of the time, Pallas kernels for 27%

profile of v4, /device:TPU:1, one launch (start us, length us, event | category | flops | bytes accessed | tf_op | source)
XLA Modules:
  0.0 192.6 jit_solution(15140345772430172039)
XLA Ops:
  7.9 0.8 broadcast_in_dim.44
  8.7 6.9 %all-to-all-start = ((bf16[16,2,128,48]{2,3,1,0:T(8,128)(2,1)}), bf16[16,2,128,48]{2,3,1,0:T(8,128)(2,1)S(1)}, u32[]{:S(2)}, u32[]{:S(2)}) async-start(bf16[16,2,128,48]{2,3,1,0:T(8,128)(2,1)} %broadcast_in_dim.44), calls=%async_computation | async-start | bytes 786432 | tf_op jit(solution)/shard_map/all_to_all | solution.py:145
  15.6 17.5 %shard_map.136 = bf16[128,16,256]{2,1,0:T(8,128)(2,1)} custom-call(bf16[128,256,128]{2,1,0:T(8,128)(2,1)} %pair_ref.3, f32[1,128]{1,0:T(1,128)} %bitcast.108, bf16[16,128]{1,0:T(8,128)(2,1)} %bitcast.101), custom_call_target="tpu_custom_call" | custom-call | tf_op jit(solution)/shard_map/pallas_call | solution.py:40
  33.1 2.6 %copy.35 = bf16[128,16,256]{2,0,1:T(8,128)(2,1)} copy(bf16[128,16,256]{2,1,0:T(8,128)(2,1)} %shard_map.136) | data formatting | bytes 2097152 | tf_op jit(solution)/shard_map/pallas_call | solution.py:40
  35.7 7.2 %all-to-all-start.1 = ((bf16[128,16,256]{2,0,1:T(8,128)(2,1)}), bf16[128,16,256]{2,0,1:T(8,128)(2,1)S(1)}, u32[]{:S(2)}, u32[]{:S(2)}) async-start(bf16[128,16,256]{2,0,1:T(8,128)(2,1)} %copy.35), calls=%async_computation.1 | async-start | bytes 2097152 | tf_op jit(solution)/shard_map/all_to_all | solution.py:153
  43.1 0.8 fusion
  44.4 0.8 reshape_squeeze.6
  45.3 0.8 reshape_squeeze.7
  46.0 11.7 %all-to-all-done.1 = bf16[128,16,256]{2,0,1:T(8,128)(2,1)S(1)} async-done(((bf16[128,16,256]{2,0,1:T(8,128)(2,1)}), bf16[128,16,256]{2,0,1:T(8,128)(2,1)S(1)}, u32[]{:S(2)}, u32[]{:S(2)}) %all-to-all-start.1) | async-done | bytes 1048608 | tf_op jit(solution)/shard_map/all_to_all | solution.py:153
  58.2 3.0 %select_reduce_fusion.1 = (f32[2,128]{1,0:T(2,128)S(1)}, f32[2,128,2048]{1,2,0:T(8,128)S(1)}, f32[2,2048,128]{2,1,0:T(8,128)}) fusion(pred[128,2048]{0,1:T(8,128)(4,1)S(1)} %copy.34, f32[128,8,2,256]{0,3,1,2:T(8,128)S(1)} %copy.36, bf16[2048,2,24]{0,2,1:T(8,128)(2,1)} %reshape_squeeze.6, bf16[128,2,24]{0,2,1:T(8,128)(2,1)S(1)} %bitcast.88), kind=kOutput, calls=%fused_computation.17 | convolution fusion | flops 27262720 | bytes 6763520 | tf_op jit(solution)/shard_map/qhd,khd->hqk/dot_general | solution.py:173
  63.2 2.1 %fusion.7 = (bf16[2,128,2048]{1,2,0:T(8,128)(2,1)S(1)}, f32[2,2048,128]{2,1,0:T(8,128)}) fusion(f32[2,128]{1,0:T(2,128)S(1)} %bitcast.107, f32[2,128,2048]{1,2,0:T(8,128)S(1)} %get-tuple-element.25, f32[2,128]{1,0:T(2,128)S(1)} %log_add_fusion, pred[128,2048]{0,1:T(8,128)(4,1)S(1)} %copy.34, bf16[2048,2,24]{0,2,1:T(8,128)(2,1)S(1)} %copy-done.2, ...), kind=kOutput, calls=%fused_computation.14 | convolution fusion | flops 28835840 | bytes 5715968 | tf_op jit(solution)/shard_map/qhd,khd->hqk/dot_general | solution.py:186
  65.9 1.0 pad_maximum_fusion
  67.0 2.9 %fusion.2 = bf16[128,2,2048]{0,2,1:T(8,128)(2,1)S(1)} fusion(f32[2,2048,128]{2,1,0:T(8,128)} %get-tuple-element.32, f32[128,8,2,256]{0,3,1,2:T(8,128)S(1)} %copy.36, f32[2,2048,128]{2,1,0:T(8,128)} %get-tuple-element.30, f32[128,2]{0,1:T(2,128)S(1)} %fusion.13, f32[128,2]{0,1:T(2,128)S(1)} %bitcast.100, pred[128,2048]{0,1:T(8,128)(4,1)S(1)} %copy.34), kind=kLoop, calls=%fused_computation.7 | loop fusion | flops 4194304 | bytes 7604224 | tf_op jit(solution)/shard_map/convert_element_type | solution.py:189
  69.9 9.5 %copy.43 = bf16[128,2,2048]{0,1,2:T(2,128)(2,1)} copy(bf16[128,2,2048]{0,2,1:T(8,128)(2,1)S(1)} %fusion.2) | data formatting | bytes 2097152 | tf_op jit(solution)/shard_map/convert_element_type | solution.py:189
  79.3 5.3 %all-to-all-start.2 = ((bf16[128,2,2048]{0,1,2:T(2,128)(2,1)}), bf16[128,2,2048]{0,1,2:T(2,128)(2,1)S(1)}, u32[]{:S(2)}, u32[]{:S(2)}) async-start(bf16[128,2,2048]{0,1,2:T(2,128)(2,1)} %copy.43), calls=%async_computation.3 | async-start | bytes 2097152 | tf_op jit(solution)/shard_map/all_to_all | solution.py:191
  84.7 0.9 fusion.12
  85.5 14.3 %all-to-all-done.2 = bf16[128,2,2048]{0,1,2:T(2,128)(2,1)S(1)} async-done(((bf16[128,2,2048]{0,1,2:T(2,128)(2,1)}), bf16[128,2,2048]{0,1,2:T(2,128)(2,1)S(1)}, u32[]{:S(2)}, u32[]{:S(2)}) %all-to-all-start.2) | async-done | bytes 1048608 | tf_op jit(solution)/shard_map/all_to_all | solution.py:191
  99.9 2.1 %copy.44 = bf16[128,2,8,256]{3,1,2,0:T(2,128)(2,1)S(1)} copy(bf16[128,2,8,256]{0,1,3,2:T(2,128)(2,1)S(1)} %bitcast.91) | data formatting | bytes 2097152 | tf_op jit(solution)/shard_map/all_to_all | solution.py:191
  102.0 1.2 all_to_all.28.ds_ref
  103.2 35.1 %shard_map.137 = (bf16[128,256,128]{2,1,0:T(8,128)(2,1)}, f32[16,128]{1,0:T(8,128)}, f32[1,128]{1,0:T(1,128)}) custom-call(bf16[128,256,128]{2,1,0:T(8,128)(2,1)} %pair_ref.3, bf16[128,16,256]{2,1,0:T(8,128)(2,1)} %all_to_all.28.ds_ref, f32[1,128]{1,0:T(1,128)} %bitcast.109, bf16[16,128]{1,0:T(8,128)(2,1)} %bitcast.102), custom_call_target="tpu_custom_call" | custom-call | tf_op jit(solution)/shard_map/pallas_call | solution.py:102
  138.3 0.8 copy.45
  139.9 19.6 %psum.7 = f32[1,2176]{1,0:T(1,128)S(1)} all-reduce(f32[1,2176]{1,0:T(1,128)S(1)} %all_gather.6), channel_id=1, replica_groups=mesh['blk'=16,'col'=8] {'col'}, use_global_device_ids=true, to_apply=%region_4.5 | all-reduce | flops 2176 | bytes 17408 | tf_op jit(solution)/shard_map/psum | solution.py:231
  159.5 23.5 %all-gather = f32[16,1,2176]{2,1,0:T(1,128)S(1)} all-gather(f32[1,1,2176]{2,1,0:T(1,128)S(1)} %bitcast.99), channel_id=1, replica_groups=mesh['blk'=16,'col'=8] {'blk'}, dimensions={0}, use_global_device_ids=true | all-gather | bytes 147968 | tf_op jit(solution)/shard_map/all_gather | solution.py:231
  184.4 0.8 convert.11
  (39 shorter events, 7.4 us)
Async XLA Ops:
  7.2 51.1 %copy-start = (bf16[128,48]{0,1:T(8,128)(2,1)S(1)}, bf16[128,48]{0,1:T(8,128)(2,1)}, u32[]{:S(2)}) copy-start(bf16[128,48]{0,1:T(8,128)(2,1)} %param.9) | copy-start | bytes 36868
  8.7 27.0 %all-to-all-start = ((bf16[16,2,128,48]{2,3,1,0:T(8,128)(2,1)}), bf16[16,2,128,48]{2,3,1,0:T(8,128)(2,1)S(1)}, u32[]{:S(2)}, u32[]{:S(2)}) async-start(bf16[16,2,128,48]{2,3,1,0:T(8,128)(2,1)} %broadcast_in_dim.44), calls=%async_computation | async-start | bytes 786432 | tf_op jit(solution)/shard_map/all_to_all | solution.py:145
  33.1 9.8 %copy-start.4 = (s32[2048]{0:T(1024)S(1)}, s32[2048]{0:T(1024)}, u32[]{:S(2)}) copy-start(s32[2048]{0:T(1024)} %param.16) | copy-start | bytes 24580
  33.1 9.9 %copy-start.5 = (s32[16,16]{1,0:T(8,128)S(1)}, s32[16,16]{1,0:T(8,128)}, u32[]{:S(2)}) copy-start(s32[16,16]{1,0:T(8,128)} %param.17) | copy-start | bytes 3076
  35.7 22.0 %all-to-all-start.1 = ((bf16[128,16,256]{2,0,1:T(8,128)(2,1)}), bf16[128,16,256]{2,0,1:T(8,128)(2,1)S(1)}, u32[]{:S(2)}, u32[]{:S(2)}) async-start(bf16[128,16,256]{2,0,1:T(8,128)(2,1)} %copy.35), calls=%async_computation.1 | async-start | bytes 2097152 | tf_op jit(solution)/shard_map/all_to_all | solution.py:153
  42.9 141.5 %reduce-scatter.2.cloned.1.call-start = ((), (), s32[]{:S(2)}) async-start(), calls=%async_computation.4 | async-start | bytes 835584 | tf_op jit(solution)/shard_map/reduce_scatter | solution.py:214
  61.2 0.7 copy-start.3
  61.2 1.4 copy-start.2
  69.9 14.8 %copy-start.1 = (bf16[2048,2,24]{0,2,1:T(8,128)(2,1)S(1)}, bf16[2048,2,24]{0,2,1:T(8,128)(2,1)}, u32[]{:S(2)}) copy-start(bf16[2048,2,24]{0,2,1:T(8,128)(2,1)} %reshape_squeeze.6) | copy-start | bytes 589828
  79.3 20.6 %all-to-all-start.2 = ((bf16[128,2,2048]{0,1,2:T(2,128)(2,1)}), bf16[128,2,2048]{0,1,2:T(2,128)(2,1)S(1)}, u32[]{:S(2)}, u32[]{:S(2)}) async-start(bf16[128,2,2048]{0,1,2:T(2,128)(2,1)} %copy.43), calls=%async_computation.3 | async-start | bytes 2097152 | tf_op jit(solution)/shard_map/all_to_all | solution.py:191
Sparse Core Ops, SparseCore 0:
  67.1 59.1 reduce-scatter.1

commit v5 on v4

--- a/solution.py
+++ b/solution.py
@@ -9,7 +9,7 @@
 
 HEAD_DIM = 24
 MASK_BLOCK = 128
-ROWS_PER_STEP = 8
+ROWS_PER_STEP = 16
 CHUNKS = 1
 
 
@@ -29,7 +29,7 @@
         bias = lax.dot_general(
             wt, normed, (((1,), (1,)), ((), ())), preferred_element_type=jnp.float32
         )
-        bias_ref[r] = bias.astype(jnp.bfloat16)
+        bias_ref[:, r, :] = bias.astype(jnp.bfloat16)
 
 
 def pair_bias(pair_rep, norm_gain, bias_weight, first, count):
@@ -39,14 +39,14 @@
     base = first // step
     return pl.pallas_call(
         _bias_kernel,
-        out_shape=jax.ShapeDtypeStruct((count, heads, cols), jnp.bfloat16),
+        out_shape=jax.ShapeDtypeStruct((heads, count, cols), jnp.bfloat16),
         grid=(count // step,),
         in_specs=[
             pl.BlockSpec((step, cols, width), lambda i: (i + base, 0, 0)),
             pl.BlockSpec((1, width), lambda i: (0, 0)),
             pl.BlockSpec((heads, width), lambda i: (0, 0)),
         ],
-        out_specs=pl.BlockSpec((step, heads, cols), lambda i: (i, 0, 0)),
+        out_specs=pl.BlockSpec((heads, step, cols), lambda i: (0, i, 0)),
         compiler_params=pltpu.CompilerParams(dimension_semantics=("arbitrary",)),
     )(pair_rep, norm_gain.reshape(1, width).astype(jnp.float32), bias_weight.T)
 
@@ -65,7 +65,7 @@
     gg = jnp.zeros(gg_ref.shape, jnp.float32)
     for r in range(pair_ref.shape[0]):
         unit, inverse, normed = _norm_rows(pair_ref[r].astype(jnp.float32), gain)
-        ds = ds_ref[r]
+        ds = ds_ref[:, r, :]
         ds_t = ds.astype(jnp.float32).T.astype(jnp.bfloat16)
         dnormed = jnp.dot(ds_t, wt, preferred_element_type=jnp.float32)
         gw = gw + jnp.dot(ds, normed, preferred_element_type=jnp.float32)
@@ -83,14 +83,14 @@
 
 def pair_grads(pair_rep, dbias, norm_gain, bias_weight, first, into):
     rows, cols, width = pair_rep.shape
-    count = dbias.shape[0]
+    count = dbias.shape[1]
     heads = bias_weight.shape[1]
     step = ROWS_PER_STEP
     base = first // step
     operands = [pair_rep, dbias, norm_gain.reshape(1, width).astype(jnp.float32), bias_weight.T]
     in_specs = [
         pl.BlockSpec((step, cols, width), lambda i: (i + base, 0, 0)),
-        pl.BlockSpec((step, heads, cols), lambda i: (i, 0, 0)),
+        pl.BlockSpec((heads, step, cols), lambda i: (0, i, 0)),
         pl.BlockSpec((1, width), lambda i: (0, 0)),
         pl.BlockSpec((heads, width), lambda i: (0, 0)),
     ]
@@ -150,8 +150,14 @@
     bias_parts = []
     for first in firsts:
         bias_local = pair_bias(pair_rep, norm_gain, bias_weight, first, count)
-        bias_mine = lax.all_to_all(bias_local, "col", split_axis=1, concat_axis=2, tiled=True)
-        bias_parts.append(jnp.transpose(bias_mine, (1, 0, 2)))
+        heads, _, cols = bias_local.shape
+        groups = lax.axis_size("col")
+        bias_mine = lax.all_to_all(
+            bias_local.reshape(groups, heads // groups, count, cols),
+            "col", split_axis=0, concat_axis=0, tiled=True,
+        )
+        bias_mine = jnp.transpose(bias_mine, (1, 2, 0, 3)).reshape(local_heads, count, all_tokens)
+        bias_parts.append(bias_mine)
 
     column_table = block_onehot(0, all_tokens, nblocks)
     query_grads, kv_parts, dbias_parts = [], [], []
@@ -187,11 +193,12 @@
             "qhd,khd->hqk", grad_heads, value_heads, preferred_element_type=jnp.float32
         )
         dscores = (probs.astype(jnp.float32) * (dprobs - delta[:, :, None])).astype(jnp.bfloat16)
-        dbias_parts.append(
-            lax.all_to_all(
-                jnp.transpose(dscores, (1, 0, 2)), "col", split_axis=2, concat_axis=1, tiled=True
-            )
-        )
+        groups = lax.axis_size("col")
+        dscores_blocks = jnp.transpose(
+            dscores.reshape(local_heads, count, groups, all_tokens // groups), (2, 0, 1, 3)
+        )
+        dbias_cells = lax.all_to_all(dscores_blocks, "col", split_axis=0, concat_axis=0, tiled=True)
+        dbias_parts.append(dbias_cells.reshape(groups * local_heads, count, all_tokens // groups))
         query_grads.append(
             jnp.einsum("hqk,khd->qhd", dscores, key_heads, preferred_element_type=jnp.float32)
             * scale_factor

time: 194 us -> 174 us (0.90)
  local copies, waits for them, and re-layouts: 21.9 us -> 8.88 us
  matrix products: 8.7 us -> 5.22 us
  Pallas kernels: 52.6 us -> 50 us
    convert_element_type x1 -> x0, local copies, waits for them, and re-layouts: 9.46 us -> none  [local(): (probs.astype(jnp.float32) * (dprobs - delta[:, :, None])).astype(jnp.bfl...]
    all_to_all x2 -> x0, local copies, waits for them, and re-layouts: 3.3 us -> none  [local(): lax.all_to_all(jnp.transpose(dscores, (1, 0, 2)), 'col', split_axis=2, co...]
    pallas_call x1 -> x0, local copies, waits for them, and re-layouts: 2.56 us -> none  [pair_bias(): pl.pallas_call(_bias_kernel, out_shape=jax.ShapeDtypeStruct((count, heads...]
    dot_general x1, matrix products: 2.96 us -> 0.74 us  [local(): jnp.einsum('qhd,khd->hqk', query_heads, key_heads, preferred_element_type...]
  transfers between devices with their start and end apart: 4 -> 4, of which waited for: 2 -> 2; matrix products, arithmetic and copies ran while one was open for 12% -> 4% of each run, Pallas kernels for 27% -> 29%
where the time goes in v5:
time: 174 us
  Pallas kernels  50 us (29%)
  blocking collectives  43.2 us (25%)
  waiting for transfers between devices  27.4 us (16%)
  starting transfers between devices  19.6 us (11%)
  between operations  14.2 us (8%)
  local copies, waits for them, and re-layouts  8.88 us (5%)
  other arithmetic  5.28 us (3%)
  matrix products  5.22 us (3%)
    pallas_call x1, Pallas kernels, pair_grads(): pl.pallas_call(_grad_kernel, out_shape=(jax.ShapeDtypeStruct((rows, cols,...  33.2 us
    all_gather x1, blocking collectives, local(): packed = jnp.sum(lax.all_gather(lax.psum(packed, 'col'), 'blk'), axis=0)  23.5 us
    psum x1, blocking collectives, local(): packed = jnp.sum(lax.all_gather(lax.psum(packed, 'col'), 'blk'), axis=0)  19.7 us
    pallas_call x1, Pallas kernels, pair_bias(): pl.pallas_call(_bias_kernel, out_shape=jax.ShapeDtypeStruct((heads, count...  16.8 us
    all_to_all x1, waiting for transfers between devices, local(): lax.all_to_all(dscores_blocks, 'col', split_axis=0, concat_axis=0, tiled=...  14.3 us
    all_to_all x1, waiting for transfers between devices, local(): lax.all_to_all(bias_local.reshape(groups, heads // groups, count, cols),...  13 us
    all_to_all x1, starting transfers between devices, local(): lax.all_to_all(bias_local.reshape(groups, heads // groups, count, cols),...  7.34 us
    all_to_all x1, starting transfers between devices, local(): lax.all_to_all(kv_rep, 'blk', split_axis=0, concat_axis=0, tiled=True)  6.9 us
  transfers between devices with their start and end apart: 4, of which 2 were waited for; matrix products, arithmetic and copies ran while one was open for 4% of the time, Pallas kernels for 29%

profile of v5, /device:TPU:1, one launch (start us, length us, event | category | flops | bytes accessed | tf_op | source)
XLA Modules:
  0.0 173.8 jit_solution(16518654159769181078)
XLA Ops:
  7.2 0.7 pad_maximum_fusion.1
  7.9 0.8 broadcast_in_dim.40
  8.7 6.9 %all-to-all-start = ((bf16[16,2,128,48]{2,3,1,0:T(8,128)(2,1)}), bf16[16,2,128,48]{2,3,1,0:T(8,128)(2,1)S(1)}, u32[]{:S(2)}, u32[]{:S(2)}) async-start(bf16[16,2,128,48]{2,3,1,0:T(8,128)(2,1)} %broadcast_in_dim.40), calls=%async_computation | async-start | bytes 786432 | tf_op jit(solution)/shard_map/all_to_all | solution.py:145
  15.6 16.8 %shard_map.136 = bf16[16,128,256]{2,1,0:T(8,128)(2,1)} custom-call(bf16[128,256,128]{2,1,0:T(8,128)(2,1)} %pair_ref.3, f32[1,128]{1,0:T(1,128)} %bitcast.84, bf16[16,128]{1,0:T(8,128)(2,1)} %bitcast.75), custom_call_target="tpu_custom_call" | custom-call | tf_op jit(solution)/shard_map/pallas_call | solution.py:40
  32.4 7.3 %all-to-all-start.1 = ((bf16[8,2,128,256]{3,2,1,0:T(8,128)(2,1)}), bf16[8,2,128,256]{3,2,1,0:T(8,128)(2,1)S(1)}, u32[]{:S(2)}, u32[]{:S(2)}) async-start(bf16[8,2,128,256]{3,2,1,0:T(8,128)(2,1)} %bitcast.69), calls=%async_computation.1 | async-start | bytes 2097152 | tf_op jit(solution)/shard_map/all_to_all | solution.py:155
  39.9 0.8 fusion.5
  41.5 13.0 %all-to-all-done.1 = bf16[8,2,128,256]{3,2,1,0:T(8,128)(2,1)S(1)} async-done(((bf16[8,2,128,256]{3,2,1,0:T(8,128)(2,1)}), bf16[8,2,128,256]{3,2,1,0:T(8,128)(2,1)S(1)}, u32[]{:S(2)}, u32[]{:S(2)}) %all-to-all-start.1) | async-done | bytes 1048608 | tf_op jit(solution)/shard_map/all_to_all | solution.py:155
  54.5 1.5 convert_bitcast_fusion
  56.1 1.9 %copy.33 = f32[2,128,8,256]{1,3,2,0:T(8,128)S(1)} copy(f32[2,128,8,256]{3,1,0,2:T(8,128)} %convert_bitcast_fusion) | data formatting | bytes 4194304 | tf_op jit(solution)/shard_map/convert_element_type | solution.py:181
  58.0 0.7 select_reduce_fusion.1
  59.5 0.7 fusion.18
  60.8 0.8 fusion.4
  62.3 1.0 pad_maximum_fusion
  63.3 1.3 copy.39
  64.6 5.3 %all-to-all-start.2 = ((bf16[8,2,128,256]{3,2,1,0:T(8,128)(2,1)}), bf16[8,2,128,256]{3,2,1,0:T(8,128)(2,1)S(1)}, u32[]{:S(2)}, u32[]{:S(2)}) async-start(bf16[8,2,128,256]{3,2,1,0:T(8,128)(2,1)} %bitcast.23), calls=%async_computation.3 | async-start | bytes 2097152 | tf_op jit(solution)/shard_map/all_to_all | solution.py:200
  69.9 0.9 fusion.10
  70.8 14.3 %all-to-all-done.2 = bf16[8,2,128,256]{3,2,1,0:T(8,128)(2,1)S(1)} async-done(((bf16[8,2,128,256]{3,2,1,0:T(8,128)(2,1)}), bf16[8,2,128,256]{3,2,1,0:T(8,128)(2,1)S(1)}, u32[]{:S(2)}, u32[]{:S(2)}) %all-to-all-start.2) | async-done | bytes 1048608 | tf_op jit(solution)/shard_map/all_to_all | solution.py:200
  85.1 1.0 copy-done.1
  86.1 33.2 %shard_map.137 = (bf16[128,256,128]{2,1,0:T(8,128)(2,1)}, f32[16,128]{1,0:T(8,128)}, f32[1,128]{1,0:T(1,128)}) custom-call(bf16[128,256,128]{2,1,0:T(8,128)(2,1)} %pair_ref.3, bf16[16,128,256]{2,1,0:T(8,128)(2,1)} %bitcast.70, f32[1,128]{1,0:T(1,128)} %bitcast.85, bf16[16,128]{1,0:T(8,128)(2,1)} %bitcast.76), custom_call_target="tpu_custom_call" | custom-call | tf_op jit(solution)/shard_map/pallas_call | solution.py:102
  119.4 0.8 copy.40
  120.9 19.7 %psum.7 = f32[1,2176]{1,0:T(1,128)S(1)} all-reduce(f32[1,2176]{1,0:T(1,128)S(1)} %all_gather.6), channel_id=1, replica_groups=mesh['blk'=16,'col'=8] {'col'}, use_global_device_ids=true, to_apply=%region_4.5 | all-reduce | flops 2176 | bytes 17408 | tf_op jit(solution)/shard_map/psum | solution.py:238
  140.6 23.5 %all-gather = f32[16,1,2176]{2,1,0:T(1,128)S(1)} all-gather(f32[1,1,2176]{2,1,0:T(1,128)S(1)} %bitcast.74), channel_id=1, replica_groups=mesh['blk'=16,'col'=8] {'blk'}, dimensions={0}, use_global_device_ids=true | all-gather | bytes 147968 | tf_op jit(solution)/shard_map/all_gather | solution.py:238
  164.8 0.7 copy.41
  165.5 0.8 convert.6
  (34 shorter events, 4.9 us)
Async XLA Ops:
  7.2 50.8 %copy-start = (bf16[128,48]{0,1:T(8,128)(2,1)S(1)}, bf16[128,48]{0,1:T(8,128)(2,1)}, u32[]{:S(2)}) copy-start(bf16[128,48]{0,1:T(8,128)(2,1)} %param.9) | copy-start | bytes 36868
  8.7 23.7 %all-to-all-start = ((bf16[16,2,128,48]{2,3,1,0:T(8,128)(2,1)}), bf16[16,2,128,48]{2,3,1,0:T(8,128)(2,1)S(1)}, u32[]{:S(2)}, u32[]{:S(2)}) async-start(bf16[16,2,128,48]{2,3,1,0:T(8,128)(2,1)} %broadcast_in_dim.40), calls=%async_computation | async-start | bytes 786432 | tf_op jit(solution)/shard_map/all_to_all | solution.py:145
  32.4 7.4 %copy-start.3 = (s32[2048]{0:T(1024)S(1)}, s32[2048]{0:T(1024)}, u32[]{:S(2)}) copy-start(s32[2048]{0:T(1024)} %param.16) | copy-start | bytes 24580
  32.4 7.5 %copy-start.4 = (s32[16,16]{1,0:T(8,128)S(1)}, s32[16,16]{1,0:T(8,128)}, u32[]{:S(2)}) copy-start(s32[16,16]{1,0:T(8,128)} %param.17) | copy-start | bytes 3076
  32.4 22.1 %all-to-all-start.1 = ((bf16[8,2,128,256]{3,2,1,0:T(8,128)(2,1)}), bf16[8,2,128,256]{3,2,1,0:T(8,128)(2,1)S(1)}, u32[]{:S(2)}, u32[]{:S(2)}) async-start(bf16[8,2,128,256]{3,2,1,0:T(8,128)(2,1)} %bitcast.69), calls=%async_computation.1 | async-start | bytes 2097152 | tf_op jit(solution)/shard_map/all_to_all | solution.py:155
  39.7 125.8 %reduce-scatter.2.cloned.1.call-start = ((), (), s32[]{:S(2)}) async-start(), calls=%async_computation.4 | async-start | bytes 835584 | tf_op jit(solution)/shard_map/reduce_scatter | solution.py:221
  58.8 0.7 copy-start.2
  64.6 20.6 %all-to-all-start.2 = ((bf16[8,2,128,256]{3,2,1,0:T(8,128)(2,1)}), bf16[8,2,128,256]{3,2,1,0:T(8,128)(2,1)S(1)}, u32[]{:S(2)}, u32[]{:S(2)}) async-start(bf16[8,2,128,256]{3,2,1,0:T(8,128)(2,1)} %bitcast.23), calls=%async_computation.3 | async-start | bytes 2097152 | tf_op jit(solution)/shard_map/all_to_all | solution.py:200
  85.1 1.0 copy-start.1
Sparse Core Ops, SparseCore 0:
  63.4 59.0 reduce-scatter.1

commit v6 on v5

--- a/solution.py
+++ b/solution.py
@@ -235,7 +235,12 @@
         gain_part = gain_part + gain_add
     pair_width = gain_part.shape[1]
     packed = jnp.concatenate([gain_part[0], weight_part.T.reshape(-1)])
-    packed = jnp.sum(lax.all_gather(lax.psum(packed, "col"), "blk"), axis=0)
+    everyone = ("blk", "col")
+    devices = lax.axis_size(everyone)
+    pieces = lax.all_to_all(packed.reshape(devices, -1), everyone, 0, 0, tiled=True)
+    piece = jnp.sum(pieces, axis=0, keepdims=True)
+    spread = jnp.broadcast_to(piece, (devices, piece.shape[1]))
+    packed = lax.all_to_all(spread, everyone, 0, 0, tiled=True).reshape(-1)
     grad_gain = packed[:pair_width]
     grad_weight = packed[pair_width:].reshape(weight_part.shape[::-1])
     return (grad_queries, grad_keys, grad_values, grad_pair, grad_gain, grad_weight)

time: 174 us -> 163 us (0.937)
  waiting for transfers between devices: 27.4 us -> 21.5 us
  blocking collectives: 43.2 us -> 37.6 us
    all_to_all x0 -> x2, blocking collectives: none -> 37.6 us  [the longest x1 21.3 us: local(): lax.all_to_all(dscores_blocks, 'col', split_axis=0, concat_axis=0, tiled=...]
    all_gather x1 -> x0, blocking collectives: 23.5 us -> none  [local(): packed = jnp.sum(lax.all_gather(lax.psum(packed, 'col'), 'blk'), axis=0)]
    psum x1 -> x0, blocking collectives: 19.7 us -> none  [local(): packed = jnp.sum(lax.all_gather(lax.psum(packed, 'col'), 'blk'), axis=0)]
    all_to_all x1, waiting for transfers between devices: 14.3 us -> 8.49 us  [local(): packed = lax.all_to_all(spread, everyone, 0, 0, tiled=True).reshape(-1)]
  transfers between devices with their start and end apart: 4 -> 4, of which waited for: 2 -> 2; matrix products, arithmetic and copies ran while one was open for 4% -> 5% of each run, Pallas kernels for 29% -> 31%
where the time goes in v6:
time: 163 us; the launch traced here: 162 us
  Pallas kernels  50 us (31%)
  blocking collectives  37.6 us (23%)
  waiting for transfers between devices  21.5 us (13%)
  starting transfers between devices  18.9 us (12%)
  between operations  14.2 us (9%)
  local copies, waits for them, and re-layouts  8.7 us (5%)
  other arithmetic  6.15 us (4%)
  matrix products  5.22 us (3%)
    pallas_call x1, Pallas kernels, pair_grads(): pl.pallas_call(_grad_kernel, out_shape=(jax.ShapeDtypeStruct((rows, cols,...  33.2 us
    all_to_all x1, blocking collectives, local(): lax.all_to_all(dscores_blocks, 'col', split_axis=0, concat_axis=0, tiled=...  21.3 us
    pallas_call x1, Pallas kernels, pair_bias(): pl.pallas_call(_bias_kernel, out_shape=jax.ShapeDtypeStruct((heads, count...  16.8 us
    all_to_all x1, blocking collectives, local(): lax.all_to_all(packed.reshape(devices, -1), everyone, 0, 0, tiled=True)  16.3 us
    all_to_all x1, waiting for transfers between devices, local(): lax.all_to_all(bias_local.reshape(groups, heads // groups, count, cols),...  13 us
    all_to_all x1, waiting for transfers between devices, local(): packed = lax.all_to_all(spread, everyone, 0, 0, tiled=True).reshape(-1)  8.49 us
    all_to_all x1, starting transfers between devices, local(): lax.all_to_all(bias_local.reshape(groups, heads // groups, count, cols),...  7.34 us
    all_to_all x1, starting transfers between devices, local(): lax.all_to_all(kv_rep, 'blk', split_axis=0, concat_axis=0, tiled=True)  6.9 us
  transfers between devices with their start and end apart: 4, of which 2 were waited for; matrix products, arithmetic and copies ran while one was open for 5% of the time, Pallas kernels for 31%

profile of v6, /device:TPU:1, one launch (start us, length us, event | category | flops | bytes accessed | tf_op | source)
XLA Modules:
  0.0 162.3 jit_solution(2859970284372741693)
XLA Ops:
  7.2 0.7 pad_maximum_fusion.1
  7.9 0.8 broadcast_in_dim.26
  8.7 6.9 %all-to-all-start = ((bf16[16,2,128,48]{2,3,1,0:T(8,128)(2,1)}), bf16[16,2,128,48]{2,3,1,0:T(8,128)(2,1)S(1)}, u32[]{:S(2)}, u32[]{:S(2)}) async-start(bf16[16,2,128,48]{2,3,1,0:T(8,128)(2,1)} %broadcast_in_dim.26), calls=%async_computation | async-start | bytes 786432 | tf_op jit(solution)/shard_map/all_to_all | solution.py:145
  15.6 16.8 %shard_map.136 = bf16[16,128,256]{2,1,0:T(8,128)(2,1)} custom-call(bf16[128,256,128]{2,1,0:T(8,128)(2,1)} %pair_ref.3, f32[1,128]{1,0:T(1,128)} %bitcast.87, bf16[16,128]{1,0:T(8,128)(2,1)} %bitcast.78), custom_call_target="tpu_custom_call" | custom-call | tf_op jit(solution)/shard_map/pallas_call | solution.py:40
  32.4 7.3 %all-to-all-start.1 = ((bf16[8,2,128,256]{3,2,1,0:T(8,128)(2,1)}), bf16[8,2,128,256]{3,2,1,0:T(8,128)(2,1)S(1)}, u32[]{:S(2)}, u32[]{:S(2)}) async-start(bf16[8,2,128,256]{3,2,1,0:T(8,128)(2,1)} %bitcast.70), calls=%async_computation.1 | async-start | bytes 2097152 | tf_op jit(solution)/shard_map/all_to_all | solution.py:155
  39.9 0.8 fusion.5
  41.5 13.0 %all-to-all-done.1 = bf16[8,2,128,256]{3,2,1,0:T(8,128)(2,1)S(1)} async-done(((bf16[8,2,128,256]{3,2,1,0:T(8,128)(2,1)}), bf16[8,2,128,256]{3,2,1,0:T(8,128)(2,1)S(1)}, u32[]{:S(2)}, u32[]{:S(2)}) %all-to-all-start.1) | async-done | bytes 1048608 | tf_op jit(solution)/shard_map/all_to_all | solution.py:155
  54.5 1.5 convert_bitcast_fusion
  56.1 1.9 %copy.33 = f32[2,128,8,256]{1,3,2,0:T(8,128)S(1)} copy(f32[2,128,8,256]{3,1,0,2:T(8,128)} %convert_bitcast_fusion) | data formatting | bytes 4194304 | tf_op jit(solution)/shard_map/convert_element_type | solution.py:181
  58.0 0.7 select_reduce_fusion.1
  59.5 0.7 fusion.18
  60.8 0.8 fusion.4
  62.3 1.0 pad_maximum_fusion
  63.8 21.3 %all_to_all.30 = bf16[8,2,128,256]{3,2,1,0:T(8,128)(2,1)} all-to-all(bf16[8,2,128,256]{3,2,1,0:T(8,128)(2,1)S(1)} %bitcast.72), channel_id=1, replica_groups=mesh['blk'=16,'col'=8] {'col'}, dimensions={0} | all-to-all | bytes 2097152 | tf_op jit(solution)/shard_map/all_to_all | solution.py:200
  85.2 33.2 %shard_map.137 = (bf16[128,256,128]{2,1,0:T(8,128)(2,1)}, f32[16,128]{1,0:T(8,128)}, f32[1,128]{1,0:T(1,128)}) custom-call(bf16[128,256,128]{2,1,0:T(8,128)(2,1)} %pair_ref.3, bf16[16,128,256]{2,1,0:T(8,128)(2,1)} %bitcast.71, f32[1,128]{1,0:T(1,128)} %bitcast.88, bf16[16,128]{1,0:T(8,128)(2,1)} %bitcast.79), custom_call_target="tpu_custom_call" | custom-call | tf_op jit(solution)/shard_map/pallas_call | solution.py:102
  118.4 0.8 copy.40
  119.3 0.7 pad_maximum_fusion.2
  120.1 16.3 %all_to_all.31 = f32[128,1,17]{2,1,0:T(1,128)S(1)} all-to-all(f32[128,1,17]{2,1,0:T(1,128)S(1)} %bitcast.77), channel_id=1, replica_groups=mesh['blk'=16,'col'=8] {'blk','col'}, dimensions={0} | all-to-all | bytes 17408 | tf_op jit(solution)/shard_map/all_to_all | solution.py:240
  137.2 4.6 %all-to-all-start.4 = ((f32[128,1,17]{2,1,0:T(1,128)}), f32[128,1,17]{2,1,0:T(1,128)S(1)}, u32[]{:S(2)}, u32[]{:S(2)}) async-start(f32[128,1,17]{2,1,0:T(1,128)} %broadcast_in_dim.50), calls=%async_computation.5 | async-start | bytes 131072 | tf_op jit(solution)/shard_map/all_to_all | solution.py:243
  141.8 0.9 fusion.10
  142.7 8.5 %all-to-all-done.4 = f32[128,1,17]{2,1,0:T(1,128)S(1)} async-done(((f32[128,1,17]{2,1,0:T(1,128)}), f32[128,1,17]{2,1,0:T(1,128)S(1)}, u32[]{:S(2)}, u32[]{:S(2)}) %all-to-all-start.4) | async-done | bytes 8736 | tf_op jit(solution)/shard_map/all_to_all | solution.py:243
  151.7 0.8 reduce.6
  153.4 0.7 copy.42
  154.0 0.8 convert.6
  (36 shorter events, 6.5 us)
Async XLA Ops:
  7.2 50.8 %copy-start = (bf16[128,48]{0,1:T(8,128)(2,1)S(1)}, bf16[128,48]{0,1:T(8,128)(2,1)}, u32[]{:S(2)}) copy-start(bf16[128,48]{0,1:T(8,128)(2,1)} %param.9) | copy-start | bytes 36868
  8.7 23.7 %all-to-all-start = ((bf16[16,2,128,48]{2,3,1,0:T(8,128)(2,1)}), bf16[16,2,128,48]{2,3,1,0:T(8,128)(2,1)S(1)}, u32[]{:S(2)}, u32[]{:S(2)}) async-start(bf16[16,2,128,48]{2,3,1,0:T(8,128)(2,1)} %broadcast_in_dim.26), calls=%async_computation | async-start | bytes 786432 | tf_op jit(solution)/shard_map/all_to_all | solution.py:145
  32.4 7.4 %copy-start.2 = (s32[2048]{0:T(1024)S(1)}, s32[2048]{0:T(1024)}, u32[]{:S(2)}) copy-start(s32[2048]{0:T(1024)} %param.16) | copy-start | bytes 24580
  32.4 7.5 %copy-start.3 = (s32[16,16]{1,0:T(8,128)S(1)}, s32[16,16]{1,0:T(8,128)}, u32[]{:S(2)}) copy-start(s32[16,16]{1,0:T(8,128)} %param.17) | copy-start | bytes 3076
  32.4 22.1 %all-to-all-start.1 = ((bf16[8,2,128,256]{3,2,1,0:T(8,128)(2,1)}), bf16[8,2,128,256]{3,2,1,0:T(8,128)(2,1)S(1)}, u32[]{:S(2)}, u32[]{:S(2)}) async-start(bf16[8,2,128,256]{3,2,1,0:T(8,128)(2,1)} %bitcast.70), calls=%async_computation.1 | async-start | bytes 2097152 | tf_op jit(solution)/shard_map/all_to_all | solution.py:155
  39.7 114.3 %reduce-scatter.2.cloned.1.call-start = ((), (), s32[]{:S(2)}) async-start(), calls=%async_computation.6 | async-start | bytes 835584 | tf_op jit(solution)/shard_map/reduce_scatter | solution.py:221
  58.8 0.7 copy-start.1
  137.2 14.0 %all-to-all-start.4 = ((f32[128,1,17]{2,1,0:T(1,128)}), f32[128,1,17]{2,1,0:T(1,128)S(1)}, u32[]{:S(2)}, u32[]{:S(2)}) async-start(f32[128,1,17]{2,1,0:T(1,128)} %broadcast_in_dim.50), calls=%async_computation.5 | async-start | bytes 131072 | tf_op jit(solution)/shard_map/all_to_all | solution.py:243
Sparse Core Ops, SparseCore 0:
  63.4 59.1 reduce-scatter.1

commit v7 on v5

--- a/solution.py
+++ b/solution.py
@@ -235,7 +235,10 @@
         gain_part = gain_part + gain_add
     pair_width = gain_part.shape[1]
     packed = jnp.concatenate([gain_part[0], weight_part.T.reshape(-1)])
-    packed = jnp.sum(lax.all_gather(lax.psum(packed, "col"), "blk"), axis=0)
+    everyone = ("blk", "col")
+    devices = lax.axis_size(everyone)
+    spread = jnp.broadcast_to(packed[None], (devices, packed.shape[0]))
+    packed = jnp.sum(lax.all_to_all(spread, everyone, 0, 0, tiled=True), axis=0)
     grad_gain = packed[:pair_width]
     grad_weight = packed[pair_width:].reshape(weight_part.shape[::-1])
     return (grad_queries, grad_keys, grad_values, grad_pair, grad_gain, grad_weight)

time: 174 us -> 156 us (0.90)
  blocking collectives: 43.2 us -> 0 us
  waiting for transfers between devices: 27.4 us -> 41.7 us
  starting transfers between devices: 19.6 us -> 28.3 us
    all_gather x1 -> x0, blocking collectives: 23.5 us -> none  [local(): packed = jnp.sum(lax.all_gather(lax.psum(packed, 'col'), 'blk'), axis=0)]
    psum x1 -> x0, blocking collectives: 19.7 us -> none  [local(): packed = jnp.sum(lax.all_gather(lax.psum(packed, 'col'), 'blk'), axis=0)]
    all_to_all x0 -> x1, waiting for transfers between devices: none -> 13.8 us  [local(): packed = jnp.sum(lax.all_to_all(spread, everyone, 0, 0, tiled=True), axis=0)]
    all_to_all x0 -> x1, starting transfers between devices: none -> 8.71 us  [local(): packed = jnp.sum(lax.all_to_all(spread, everyone, 0, 0, tiled=True), axis=0)]
    reduce_scatter x1, waiting for transfers between devices: 0.01 us -> 2.17 us  [local(): kv_grads = lax.psum_scatter(kv_part, 'blk', scatter_dimension=1, tiled=True)]
  transfers between devices with their start and end apart: 4 -> 5, of which waited for: 2 -> 4; matrix products, arithmetic and copies ran while one was open for 4% -> 6% of each run, Pallas kernels for 29% -> 32%
where the time goes in v7:
time: 156 us
  Pallas kernels  50 us (32%)
  waiting for transfers between devices  41.7 us (27%)
  starting transfers between devices  28.3 us (18%)
  between operations  14.2 us (9%)
  local copies, waits for them, and re-layouts  10.4 us (7%)
  other arithmetic  5.87 us (4%)
  matrix products  5.22 us (3%)
    pallas_call x1, Pallas kernels, pair_grads(): pl.pallas_call(_grad_kernel, out_shape=(jax.ShapeDtypeStruct((rows, cols,...  33.2 us
    pallas_call x1, Pallas kernels, pair_bias(): pl.pallas_call(_bias_kernel, out_shape=jax.ShapeDtypeStruct((heads, count...  16.8 us
    all_to_all x1, waiting for transfers between devices, local(): packed = jnp.sum(lax.all_to_all(spread, everyone, 0, 0, tiled=True), axis=0)  13.8 us
    all_to_all x1, waiting for transfers between devices, local(): lax.all_to_all(bias_local.reshape(groups, heads // groups, count, cols),...  13.1 us
    all_to_all x1, waiting for transfers between devices, local(): lax.all_to_all(dscores_blocks, 'col', split_axis=0, concat_axis=0, tiled=...  12.7 us
    all_to_all x1, starting transfers between devices, local(): packed = jnp.sum(lax.all_to_all(spread, everyone, 0, 0, tiled=True), axis=0)  8.71 us
    all_to_all x1, starting transfers between devices, local(): lax.all_to_all(bias_local.reshape(groups, heads // groups, count, cols),...  7.34 us
    all_to_all x1, starting transfers between devices, local(): lax.all_to_all(kv_rep, 'blk', split_axis=0, concat_axis=0, tiled=True)  6.9 us
  transfers between devices with their start and end apart: 5, of which 4 were waited for; matrix products, arithmetic and copies ran while one was open for 6% of the time, Pallas kernels for 32%

profile of v7, /device:TPU:1, one launch (start us, length us, event | category | flops | bytes accessed | tf_op | source)
XLA Modules:
  0.0 155.8 jit_solution(7924013381127204159)
XLA Ops:
  7.2 0.7 pad_maximum_fusion.1
  7.9 0.8 broadcast_in_dim.26
  8.7 6.9 %all-to-all-start = ((bf16[16,2,128,48]{2,3,1,0:T(8,128)(2,1)}), bf16[16,2,128,48]{2,3,1,0:T(8,128)(2,1)S(1)}, u32[]{:S(2)}, u32[]{:S(2)}) async-start(bf16[16,2,128,48]{2,3,1,0:T(8,128)(2,1)} %broadcast_in_dim.26), calls=%async_computation | async-start | bytes 786432 | tf_op jit(solution)/shard_map/all_to_all | solution.py:145
  15.6 16.8 %shard_map.136 = bf16[16,128,256]{2,1,0:T(8,128)(2,1)} custom-call(bf16[128,256,128]{2,1,0:T(8,128)(2,1)} %pair_ref.3, f32[1,128]{1,0:T(1,128)} %bitcast.82, bf16[16,128]{1,0:T(8,128)(2,1)} %bitcast.73), custom_call_target="tpu_custom_call" | custom-call | tf_op jit(solution)/shard_map/pallas_call | solution.py:40
  32.4 7.3 %all-to-all-start.1 = ((bf16[8,2,128,256]{3,2,1,0:T(8,128)(2,1)}), bf16[8,2,128,256]{3,2,1,0:T(8,128)(2,1)S(1)}, u32[]{:S(2)}, u32[]{:S(2)}) async-start(bf16[8,2,128,256]{3,2,1,0:T(8,128)(2,1)} %bitcast.68), calls=%async_computation.1 | async-start | bytes 2097152 | tf_op jit(solution)/shard_map/all_to_all | solution.py:155
  39.9 0.8 fusion.5
  41.5 13.1 %all-to-all-done.1 = bf16[8,2,128,256]{3,2,1,0:T(8,128)(2,1)S(1)} async-done(((bf16[8,2,128,256]{3,2,1,0:T(8,128)(2,1)}), bf16[8,2,128,256]{3,2,1,0:T(8,128)(2,1)S(1)}, u32[]{:S(2)}, u32[]{:S(2)}) %all-to-all-start.1) | async-done | bytes 1048608 | tf_op jit(solution)/shard_map/all_to_all | solution.py:155
  54.5 1.5 convert_bitcast_fusion
  56.1 1.9 %copy.55 = f32[2,128,8,256]{1,3,2,0:T(8,128)S(1)} copy(f32[2,128,8,256]{3,1,0,2:T(8,128)} %convert_bitcast_fusion) | data formatting | bytes 4194304 | tf_op jit(solution)/shard_map/convert_element_type | solution.py:181
  58.0 0.7 select_reduce_fusion.1
  60.8 0.8 fusion.4
  61.6 1.3 copy.61
  62.9 5.3 %all-to-all-start.2 = ((bf16[8,2,128,256]{3,2,1,0:T(8,128)(2,1)}), bf16[8,2,128,256]{3,2,1,0:T(8,128)(2,1)S(1)}, u32[]{:S(2)}, u32[]{:S(2)}) async-start(bf16[8,2,128,256]{3,2,1,0:T(8,128)(2,1)} %bitcast.23), calls=%async_computation.3 | async-start | bytes 2097152 | tf_op jit(solution)/shard_map/all_to_all | solution.py:200
  69.0 1.0 pad_maximum_fusion
  70.0 12.7 %all-to-all-done.2 = bf16[8,2,128,256]{3,2,1,0:T(8,128)(2,1)S(1)} async-done(((bf16[8,2,128,256]{3,2,1,0:T(8,128)(2,1)}), bf16[8,2,128,256]{3,2,1,0:T(8,128)(2,1)S(1)}, u32[]{:S(2)}, u32[]{:S(2)}) %all-to-all-start.2) | async-done | bytes 1048608 | tf_op jit(solution)/shard_map/all_to_all | solution.py:200
  82.7 1.0 copy-done.1
  83.7 33.2 %shard_map.137 = (bf16[128,256,128]{2,1,0:T(8,128)(2,1)}, f32[16,128]{1,0:T(8,128)}, f32[1,128]{1,0:T(1,128)}) custom-call(bf16[128,256,128]{2,1,0:T(8,128)(2,1)} %pair_ref.3, bf16[16,128,256]{2,1,0:T(8,128)(2,1)} %bitcast.69, f32[1,128]{1,0:T(1,128)} %bitcast.83, bf16[16,128]{1,0:T(8,128)(2,1)} %bitcast.74), custom_call_target="tpu_custom_call" | custom-call | tf_op jit(solution)/shard_map/pallas_call | solution.py:102
  116.9 0.8 copy.62
  118.4 1.6 %broadcast_in_dim.50 = f32[128,1,2176]{2,1,0:T(1,128)} broadcast(f32[2176]{0:T(1024)S(1)} %pad_maximum_fusion.2), dimensions={2} | broadcast | bytes 1122816 | tf_op jit(solution)/shard_map/broadcast_in_dim | solution.py:240
  120.0 8.7 %all-to-all-start.3 = ((f32[128,1,2176]{2,1,0:T(1,128)}), f32[128,1,2176]{2,1,0:T(1,128)S(1)}, u32[]{:S(2)}, u32[]{:S(2)}) async-start(f32[128,1,2176]{2,1,0:T(1,128)} %broadcast_in_dim.50), calls=%async_computation.4 | async-start | bytes 2228224 | tf_op jit(solution)/shard_map/all_to_all | solution.py:241
  128.7 0.9 fusion.10
  129.6 2.2 %reduce-scatter.2.cloned.1.call-done = f32[2,128,48]{1,2,0:T(8,128)} async-done(((f32[2,2048,48]{1,2,0:T(8,128)}), f32[2,128,48]{1,2,0:T(8,128)}) %reduce-scatter.2.cloned.1.call-update) | async-done | bytes 49168 | tf_op jit(solution)/shard_map/reduce_scatter | solution.py:221
  131.8 0.8 convert.6
  133.2 13.8 %all-to-all-done.3 = f32[128,1,2176]{2,1,0:T(1,128)S(1)} async-done(((f32[128,1,2176]{2,1,0:T(1,128)}), f32[128,1,2176]{2,1,0:T(1,128)S(1)}, u32[]{:S(2)}, u32[]{:S(2)}) %all-to-all-start.3) | async-done | bytes 1114144 | tf_op jit(solution)/shard_map/all_to_all | solution.py:241
  (34 shorter events, 6.9 us)
Async XLA Ops:
  7.2 50.9 %copy-start = (bf16[128,48]{0,1:T(8,128)(2,1)S(1)}, bf16[128,48]{0,1:T(8,128)(2,1)}, u32[]{:S(2)}) copy-start(bf16[128,48]{0,1:T(8,128)(2,1)} %param.9) | copy-start | bytes 36868
  8.7 23.7 %all-to-all-start = ((bf16[16,2,128,48]{2,3,1,0:T(8,128)(2,1)}), bf16[16,2,128,48]{2,3,1,0:T(8,128)(2,1)S(1)}, u32[]{:S(2)}, u32[]{:S(2)}) async-start(bf16[16,2,128,48]{2,3,1,0:T(8,128)(2,1)} %broadcast_in_dim.26), calls=%async_computation | async-start | bytes 786432 | tf_op jit(solution)/shard_map/all_to_all | solution.py:145
  32.4 7.4 %copy-start.3 = (s32[2048]{0:T(1024)S(1)}, s32[2048]{0:T(1024)}, u32[]{:S(2)}) copy-start(s32[2048]{0:T(1024)} %param.16) | copy-start | bytes 24580
  32.4 7.5 %copy-start.4 = (s32[16,16]{1,0:T(8,128)S(1)}, s32[16,16]{1,0:T(8,128)}, u32[]{:S(2)}) copy-start(s32[16,16]{1,0:T(8,128)} %param.17) | copy-start | bytes 3076
  32.4 22.1 %all-to-all-start.1 = ((bf16[8,2,128,256]{3,2,1,0:T(8,128)(2,1)}), bf16[8,2,128,256]{3,2,1,0:T(8,128)(2,1)S(1)}, u32[]{:S(2)}, u32[]{:S(2)}) async-start(bf16[8,2,128,256]{3,2,1,0:T(8,128)(2,1)} %bitcast.68), calls=%async_computation.1 | async-start | bytes 2097152 | tf_op jit(solution)/shard_map/all_to_all | solution.py:155
  58.8 0.7 copy-start.2
  62.9 19.8 %all-to-all-start.2 = ((bf16[8,2,128,256]{3,2,1,0:T(8,128)(2,1)}), bf16[8,2,128,256]{3,2,1,0:T(8,128)(2,1)S(1)}, u32[]{:S(2)}, u32[]{:S(2)}) async-start(bf16[8,2,128,256]{3,2,1,0:T(8,128)(2,1)} %bitcast.23), calls=%async_computation.3 | async-start | bytes 2097152 | tf_op jit(solution)/shard_map/all_to_all | solution.py:200
  68.3 63.5 %reduce-scatter.2.cloned.1.call-start = ((), (), s32[]{:S(2)}) async-start(), calls=%async_computation.5 | async-start | bytes 835584 | tf_op jit(solution)/shard_map/reduce_scatter | solution.py:221
  82.7 1.0 copy-start.1
  120.0 27.0 %all-to-all-start.3 = ((f32[128,1,2176]{2,1,0:T(1,128)}), f32[128,1,2176]{2,1,0:T(1,128)S(1)}, u32[]{:S(2)}, u32[]{:S(2)}) async-start(f32[128,1,2176]{2,1,0:T(1,128)} %broadcast_in_dim.50), calls=%async_computation.4 | async-start | bytes 2228224 | tf_op jit(solution)/shard_map/all_to_all | solution.py:241
Sparse Core Ops, SparseCore 0:
  71.4 60.2 reduce-scatter.1

commit v8 on v7

--- a/solution.py
+++ b/solution.py
@@ -218,7 +218,8 @@
     kv_part = kv_parts[0]
     for extra in kv_parts[1:]:
         kv_part = kv_part + extra
-    kv_grads = lax.psum_scatter(kv_part, "blk", scatter_dimension=1, tiled=True)
+    kv_blocks = kv_part.reshape(2, blk_count, tok_rows, local_width)
+    kv_grads = jnp.sum(lax.all_to_all(kv_blocks, "blk", 1, 1, tiled=True), axis=1)
     grad_queries = jnp.concatenate(query_grads, axis=0).reshape(tok_rows, local_width)
     grad_queries = grad_queries.astype(jnp.bfloat16)
     grad_keys = kv_grads[0].astype(jnp.bfloat16)

time: 156 us -> 148 us (0.949)
  between operations: 14.2 us -> 0.81 us
  starting transfers between devices: 28.3 us -> 34 us
  other arithmetic: 5.87 us -> 3.75 us
    all_to_all x0 -> x1, starting transfers between devices: none -> 6.9 us  [local(): lax.all_to_all(kv_blocks, 'blk', 1, 1, tiled=True)]
    all_to_all x1, waiting for transfers between devices: 13.8 us -> 16.7 us  [local(): packed = jnp.sum(lax.all_to_all(spread, everyone, 0, 0, tiled=True), axis=0)]
    reduce_scatter x1 -> x0, waiting for transfers between devices: 2.17 us -> none  [local(): kv_grads = lax.psum_scatter(kv_part, 'blk', scatter_dimension=1, tiled=True)]
  transfers between devices with their start and end apart: 5 -> 5, of which waited for: 4 -> 3; matrix products, arithmetic and copies ran while one was open for 6% -> 6% of each run, Pallas kernels for 32% -> 34%
where the time goes in v8:
time: 148 us; the launch traced here: 147 us
  Pallas kernels  50 us (34%)
  waiting for transfers between devices  40.2 us (27%)
  starting transfers between devices  34 us (23%)
  local copies, waits for them, and re-layouts  11.4 us (8%)
  matrix products  6.74 us (5%)
  other arithmetic  3.75 us (3%)
    pallas_call x1, Pallas kernels, pair_grads(): pl.pallas_call(_grad_kernel, out_shape=(jax.ShapeDtypeStruct((rows, cols,...  33.2 us
    pallas_call x1, Pallas kernels, pair_bias(): pl.pallas_call(_bias_kernel, out_shape=jax.ShapeDtypeStruct((heads, count...  16.8 us
    all_to_all x1, waiting for transfers between devices, local(): packed = jnp.sum(lax.all_to_all(spread, everyone, 0, 0, tiled=True), axis=0)  16.7 us
    all_to_all x1, waiting for transfers between devices, local(): lax.all_to_all(dscores_blocks, 'col', split_axis=0, concat_axis=0, tiled=...  11.8 us
    all_to_all x1, waiting for transfers between devices, local(): lax.all_to_all(bias_local.reshape(groups, heads // groups, count, cols),...  11.7 us
    all_to_all x1, starting transfers between devices, local(): packed = jnp.sum(lax.all_to_all(spread, everyone, 0, 0, tiled=True), axis=0)  7.52 us
    all_to_all x1, starting transfers between devices, local(): lax.all_to_all(bias_local.reshape(groups, heads // groups, count, cols),...  7.34 us
    all_to_all x1, starting transfers between devices, local(): lax.all_to_all(kv_rep, 'blk', split_axis=0, concat_axis=0, tiled=True)  6.9 us
  transfers between devices with their start and end apart: 5, of which 3 were waited for; matrix products, arithmetic and copies ran while one was open for 6% of the time, Pallas kernels for 34%

profile of v8, /device:TPU:1, one launch (start us, length us, event | category | flops | bytes accessed | tf_op | source)
XLA Modules:
  0.0 147.0 jit_solution(11983473890318334422)
XLA Ops:
  0.6 0.7 pad_maximum_fusion.1
  1.4 0.8 broadcast_in_dim.26
  2.2 6.9 %all-to-all-start = ((bf16[16,2,128,48]{2,3,1,0:T(8,128)(2,1)}), bf16[16,2,128,48]{2,3,1,0:T(8,128)(2,1)S(1)}, u32[]{:S(2)}, u32[]{:S(2)}) async-start(bf16[16,2,128,48]{2,3,1,0:T(8,128)(2,1)} %broadcast_in_dim.26), calls=%async_computation | async-start | bytes 786432 | tf_op jit(solution)/shard_map/all_to_all | solution.py:145
  9.1 16.8 %shard_map.136 = bf16[16,128,256]{2,1,0:T(8,128)(2,1)} custom-call(bf16[128,256,128]{2,1,0:T(8,128)(2,1)} %pair_ref.3, f32[1,128]{1,0:T(1,128)} %bitcast.92, bf16[16,128]{1,0:T(8,128)(2,1)} %bitcast.83), custom_call_target="tpu_custom_call" | custom-call | tf_op jit(solution)/shard_map/pallas_call | solution.py:40
  25.9 7.3 %all-to-all-start.1 = ((bf16[8,2,128,256]{3,2,1,0:T(8,128)(2,1)}), bf16[8,2,128,256]{3,2,1,0:T(8,128)(2,1)S(1)}, u32[]{:S(2)}, u32[]{:S(2)}) async-start(bf16[8,2,128,256]{3,2,1,0:T(8,128)(2,1)} %bitcast.76), calls=%async_computation.1 | async-start | bytes 2097152 | tf_op jit(solution)/shard_map/all_to_all | solution.py:155
  33.3 0.8 fusion.5
  34.7 0.8 reshape_squeeze.7
  35.5 0.8 reshape_squeeze.6
  36.3 11.7 %all-to-all-done.1 = bf16[8,2,128,256]{3,2,1,0:T(8,128)(2,1)S(1)} async-done(((bf16[8,2,128,256]{3,2,1,0:T(8,128)(2,1)}), bf16[8,2,128,256]{3,2,1,0:T(8,128)(2,1)S(1)}, u32[]{:S(2)}, u32[]{:S(2)}) %all-to-all-start.1) | async-done | bytes 1048608 | tf_op jit(solution)/shard_map/all_to_all | solution.py:155
  48.3 1.8 %copy.59 = f32[2,128,8,256]{1,3,2,0:T(8,128)} copy(f32[2,128,8,256]{3,1,0,2:T(8,128)S(1)} %convert_bitcast_fusion) | data formatting | bytes 4194304 | tf_op jit(solution)/shard_map/convert_element_type | solution.py:181
  50.1 2.3 %select_reduce_fusion.1 = (f32[2,128]{1,0:T(2,128)S(1)}, f32[2,128,2048]{1,2,0:T(8,128)S(1)}) fusion(pred[128,2048]{0,1:T(8,128)(4,1)S(1)} %copy.58, f32[2,128,2048]{1,2,0:T(8,128)} %bitcast.75, bf16[2048,2,24]{0,2,1:T(8,128)(2,1)S(1)} %copy-done.1, bf16[128,2,24]{0,2,1:T(8,128)(2,1)S(1)} %bitcast.72), kind=kOutput, calls=%fused_computation.13 | convolution fusion | flops 27262720 | bytes 4666368 | tf_op jit(solution)/shard_map/qhd,khd->hqk/dot_general | solution.py:179
  53.9 0.8 fusion.4
  54.7 1.3 copy.67
  56.1 5.3 %all-to-all-start.3 = ((bf16[8,2,128,256]{3,2,1,0:T(8,128)(2,1)}), bf16[8,2,128,256]{3,2,1,0:T(8,128)(2,1)}, u32[]{:S(2)}, u32[]{:S(2)}) async-start(bf16[8,2,128,256]{3,2,1,0:T(8,128)(2,1)} %bitcast.77), calls=%async_computation.3 | async-start | bytes 2097152 | tf_op jit(solution)/shard_map/all_to_all | solution.py:200
  63.2 1.0 pad_maximum_fusion
  64.1 11.8 %all-to-all-done.3 = bf16[8,2,128,256]{3,2,1,0:T(8,128)(2,1)} async-done(((bf16[8,2,128,256]{3,2,1,0:T(8,128)(2,1)}), bf16[8,2,128,256]{3,2,1,0:T(8,128)(2,1)}, u32[]{:S(2)}, u32[]{:S(2)}) %all-to-all-start.3) | async-done | bytes 1048608 | tf_op jit(solution)/shard_map/all_to_all | solution.py:200
  75.9 6.9 %all-to-all-start.2 = ((f32[2,16,128,48]{2,3,0,1:T(8,128)}), f32[2,16,128,48]{2,3,0,1:T(8,128)S(1)}, u32[]{:S(2)}, u32[]{:S(2)}) async-start(f32[2,16,128,48]{2,3,0,1:T(8,128)} %pad_maximum_fusion), calls=%async_computation.2 | async-start | bytes 1572864 | tf_op jit(solution)/shard_map/all_to_all | solution.py:222
  82.8 33.2 %shard_map.137 = (bf16[128,256,128]{2,1,0:T(8,128)(2,1)}, f32[16,128]{1,0:T(8,128)}, f32[1,128]{1,0:T(1,128)}) custom-call(bf16[128,256,128]{2,1,0:T(8,128)(2,1)} %pair_ref.3, bf16[16,128,256]{2,1,0:T(8,128)(2,1)} %bitcast.22.ds_ref, f32[1,128]{1,0:T(1,128)} %bitcast.93, bf16[16,128]{1,0:T(8,128)(2,1)} %bitcast.84), custom_call_target="tpu_custom_call" | custom-call | tf_op jit(solution)/shard_map/pallas_call | solution.py:102
  116.1 0.8 copy.68
  117.6 1.6 %broadcast_in_dim.50 = f32[128,1,2176]{2,1,0:T(1,128)} broadcast(f32[2176]{0:T(1024)S(1)} %pad_maximum_fusion.2), dimensions={2} | broadcast | bytes 1122816 | tf_op jit(solution)/shard_map/broadcast_in_dim | solution.py:241
  119.2 7.5 %all-to-all-start.4 = ((f32[128,1,2176]{2,1,0:T(1,128)}), f32[128,1,2176]{2,1,0:T(1,128)S(1)}, u32[]{:S(2)}, u32[]{:S(2)}) async-start(f32[128,1,2176]{2,1,0:T(1,128)} %broadcast_in_dim.50), calls=%async_computation.4 | async-start | bytes 2228224 | tf_op jit(solution)/shard_map/all_to_all | solution.py:242
  126.8 0.9 fusion.10
  128.3 16.7 %all-to-all-done.4 = f32[128,1,2176]{2,1,0:T(1,128)S(1)} async-done(((f32[128,1,2176]{2,1,0:T(1,128)}), f32[128,1,2176]{2,1,0:T(1,128)S(1)}, u32[]{:S(2)}, u32[]{:S(2)}) %all-to-all-start.4) | async-done | bytes 1114144 | tf_op jit(solution)/shard_map/all_to_all | solution.py:242
  145.0 0.7 reduce_sum.39
  (41 shorter events, 6.8 us)
Async XLA Ops:
  0.6 49.4 %copy-start = (bf16[128,48]{0,1:T(8,128)(2,1)S(1)}, bf16[128,48]{0,1:T(8,128)(2,1)}, u32[]{:S(2)}) copy-start(bf16[128,48]{0,1:T(8,128)(2,1)} %param.9) | copy-start | bytes 36868
  2.2 23.7 %all-to-all-start = ((bf16[16,2,128,48]{2,3,1,0:T(8,128)(2,1)}), bf16[16,2,128,48]{2,3,1,0:T(8,128)(2,1)S(1)}, u32[]{:S(2)}, u32[]{:S(2)}) async-start(bf16[16,2,128,48]{2,3,1,0:T(8,128)(2,1)} %broadcast_in_dim.26), calls=%async_computation | async-start | bytes 786432 | tf_op jit(solution)/shard_map/all_to_all | solution.py:145
  25.9 7.4 %copy-start.5 = (s32[2048]{0:T(1024)S(1)}, s32[2048]{0:T(1024)}, u32[]{:S(2)}) copy-start(s32[2048]{0:T(1024)} %param.16) | copy-start | bytes 24580
  25.9 7.5 %copy-start.6 = (s32[16,16]{1,0:T(8,128)S(1)}, s32[16,16]{1,0:T(8,128)}, u32[]{:S(2)}) copy-start(s32[16,16]{1,0:T(8,128)} %param.17) | copy-start | bytes 3076
  25.9 22.1 %all-to-all-start.1 = ((bf16[8,2,128,256]{3,2,1,0:T(8,128)(2,1)}), bf16[8,2,128,256]{3,2,1,0:T(8,128)(2,1)S(1)}, u32[]{:S(2)}, u32[]{:S(2)}) async-start(bf16[8,2,128,256]{3,2,1,0:T(8,128)(2,1)} %bitcast.76), calls=%async_computation.1 | async-start | bytes 2097152 | tf_op jit(solution)/shard_map/all_to_all | solution.py:155
  48.3 1.8 %copy-start.1 = (bf16[2048,2,24]{0,2,1:T(8,128)(2,1)S(1)}, bf16[2048,2,24]{0,2,1:T(8,128)(2,1)}, u32[]{:S(2)}) copy-start(bf16[2048,2,24]{0,2,1:T(8,128)(2,1)} %reshape_squeeze.6) | copy-start | bytes 589828
  52.4 0.9 copy-start.3
  52.4 0.9 copy-start.4
  56.1 19.9 %all-to-all-start.3 = ((bf16[8,2,128,256]{3,2,1,0:T(8,128)(2,1)}), bf16[8,2,128,256]{3,2,1,0:T(8,128)(2,1)}, u32[]{:S(2)}, u32[]{:S(2)}) async-start(bf16[8,2,128,256]{3,2,1,0:T(8,128)(2,1)} %bitcast.77), calls=%async_computation.3 | async-start | bytes 2097152 | tf_op jit(solution)/shard_map/all_to_all | solution.py:200
  75.9 41.7 %all-to-all-start.2 = ((f32[2,16,128,48]{2,3,0,1:T(8,128)}), f32[2,16,128,48]{2,3,0,1:T(8,128)S(1)}, u32[]{:S(2)}, u32[]{:S(2)}) async-start(f32[2,16,128,48]{2,3,0,1:T(8,128)} %pad_maximum_fusion), calls=%async_computation.2 | async-start | bytes 1572864 | tf_op jit(solution)/shard_map/all_to_all | solution.py:222
  116.1 10.7 %copy-start.2 = (bf16[2048,2,24]{0,2,1:T(8,128)(2,1)S(1)}, bf16[2048,2,24]{0,2,1:T(8,128)(2,1)}, u32[]{:S(2)}) copy-start(bf16[2048,2,24]{0,2,1:T(8,128)(2,1)} %reshape_squeeze.6) | copy-start | bytes 589828
  119.2 25.8 %all-to-all-start.4 = ((f32[128,1,2176]{2,1,0:T(1,128)}), f32[128,1,2176]{2,1,0:T(1,128)S(1)}, u32[]{:S(2)}, u32[]{:S(2)}) async-start(f32[128,1,2176]{2,1,0:T(1,128)} %broadcast_in_dim.50), calls=%async_computation.4 | async-start | bytes 2228224 | tf_op jit(solution)/shard_map/all_to_all | solution.py:242
